TPU v7x, 256 devices: a whole 4x4x8 slice. The times are simulated.
256 devices in a mesh: row: 8 (over z), col: 32 (over y, x, core).
Axes of the slice: x: 4, y: 4, z: 8, core: 2. Of those that a mesh axis runs over, the one named last changes fastest.
Arguments:
- hidden_in: bfloat16 [1024, 2304], P('row', 'col'), may hold values from -40 to 40
- attn_gain: float32 [2304], P('col'), may hold values from 0.1 to 1.9
- qkv_weight: bfloat16 [2304, 6912], P('col'), may hold values from -0.125 to 0.125
- out_weight: bfloat16 [2304, 2304], P(None, 'col'), may hold values from -0.125 to 0.125
- moe_gain: float32 [2304], P('col'), may hold values from 0.1 to 1.9
- router_weight: float32 [2304, 8], P('col'), may hold values from -0.125 to 0.125
- expert_gate: bfloat16 [8, 2304, 5760], P('row', None, 'col'), may hold values from -0.125 to 0.125
- expert_up: bfloat16 [8, 2304, 5760], P('row', None, 'col'), may hold values from -0.125 to 0.125
- expert_down: bfloat16 [8, 5760, 2304], P('row', 'col'), may hold values from -0.078125 to 0.078125
- cache_keys: bfloat16 [2048, 64, 2304], P(('row', 'col')), may hold values from -400 to 400
- cache_values: bfloat16 [2048, 64, 2304], P(('row', 'col')), may hold values from -12 to 12
- block_table: int32 [8, 4, 64], P('row'), may hold values from 0 to 2047, as said below
- prefix_lengths: int32 [8, 4], P('row'), may hold values from 1024 to 4096, as said below
- prompt_lengths: int32 [8, 4], P('row'), may hold values from 1 to 64, 128 in all within a row
- routed_experts: int32 [1024, 2], P('row'), may hold values from 0 to 7, all different within a row; in each aligned block of 128 rows (0 to 127, 128 to 255, ...) at most 64 rows name the same one
Outputs:
- attn_out: bfloat16 [1024, 2304], P('row', 'col')
- moe_out: bfloat16 [1024, 2304], P('row', 'col')
- layer_out: bfloat16 [1024, 2304], P('row', 'col')
Inputs may be any that keep to these rules, and one draw needn't show every extreme that they name: `block_table`: entry [g, q, j] lies among the 8 pages that begin at (g * 32 + j % 32) * 8; the entries that fall among the same 8 pages are distinct. `prefix_lengths`: some request has exactly 4096 cached tokens. `prompt_lengths`: the 4 lengths of a group sum to 128; the longest of each group is exactly 64. `routed_experts`: the 2 experts of a token differ; among the tokens of one group no expert is named more than 64 times, and in some group an expert reaches 64; every expert is named by some token.
All inputs are finite; a program needn't handle non-finite values.
Results may differ from a plain program's by a relative error of at most 0.02.
The roundings to bfloat16 on the way count: a program that leaves them out, or rounds other values in their place, can miss the bound.
Values may be sent and summed in bfloat16 or wider, within the bound.
No kernel may reach another device: no remote copies, remote signals or barrier semaphores. Data moves between devices by JAX's collectives and lax.ppermute only.
A program may use at most 192 MiB of HBM per device.

v0:
```python
import math

import jax
import jax.numpy as jnp
from jax import lax
from jax.sharding import PartitionSpec as P

D = 2304
HEAD_DIM = 64
TOP = 2


norm_epsilon = 1e-05
residual_scale = 1.4 / math.sqrt(40.0)
rotary_base = 10000.0
masked_score = -1e30


def merged(value, axis, join):
    pieces = jax.tree.map(lambda part: lax.all_gather(part, axis), value)
    head = jax.tree.map(lambda part: part[0], pieces)
    tail = jax.tree.map(lambda part: part[1:], pieces)
    running, _ = lax.scan(lambda running, slab: (join(running, slab), None), head, tail)
    return running


def rotate(values, positions, head_dim):
    row_count = values.shape[0]
    head_count = values.shape[1] // head_dim
    half_dim = head_dim // 2
    frequency = rotary_base ** (-2.0 * jnp.arange(half_dim, dtype=jnp.float32) / head_dim)
    angles = positions.astype(jnp.float32)[:, None] * frequency[None, :]
    cosine = jnp.cos(angles)[:, None, :]
    sine_part = jnp.sin(angles)[:, None, :]
    shaped = values.reshape(row_count, head_count, head_dim)
    first_half = shaped[:, :, :half_dim]
    second_half = shaped[:, :, half_dim:]
    turned = jnp.concatenate(
        [
            first_half * cosine - second_half * sine_part,
            second_half * cosine + first_half * sine_part,
        ],
        axis=2,
    )
    return turned.reshape(row_count, head_count * head_dim)


def token_layout(prompt_row, prefix_row, row_count):
    run_ends = jnp.cumsum(prompt_row, dtype=jnp.int32)
    starts = run_ends - prompt_row
    offsets = jnp.arange(row_count, dtype=jnp.int32)
    request = jnp.sum(
        (offsets[:, None] >= run_ends[None, :]).astype(jnp.int32), axis=1, dtype=jnp.int32
    )
    member = request[:, None] == jnp.arange(prompt_row.shape[0], dtype=jnp.int32)[None, :]
    start_of = jnp.sum(jnp.where(member, starts[None, :], 0), axis=1, dtype=jnp.int32)
    prefix_of = jnp.sum(jnp.where(member, prefix_row[None, :], 0), axis=1, dtype=jnp.int32)
    return (request, prefix_of + offsets - start_of)


def rescale(summed, factor):
    group_count, row_count, feature_width = summed.shape
    group_size = factor.shape[1]
    shaped = summed.reshape(group_count, row_count, group_size, feature_width // group_size)
    shaped = shaped * jnp.transpose(factor, (0, 2, 1))[:, :, :, None]
    return shaped.reshape(group_count, row_count, feature_width)


def divide_rows(summed, total_weight):
    group_count, row_count, feature_width = summed.shape
    group_size = total_weight.shape[1]
    shaped = summed.reshape(group_count, row_count, group_size, feature_width // group_size)
    shaped = shaped / jnp.transpose(total_weight, (0, 2, 1))[:, :, :, None]
    return shaped.reshape(group_count, row_count, feature_width)


def combine_parts(earlier_part, later_part):
    largest = jnp.maximum(earlier_part[0], later_part[0])
    factor_one = jnp.exp(earlier_part[0] - largest)
    factor_two = jnp.exp(later_part[0] - largest)
    total_weight = earlier_part[1] * factor_one + later_part[1] * factor_two
    summed = rescale(earlier_part[2], factor_one) + rescale(later_part[2], factor_two)
    return (largest, total_weight, summed)


def on_device(
    hidden_in,
    attn_gain,
    qkv_weight,
    out_weight,
    moe_gain,
    router_weight,
    expert_gate,
    expert_up,
    expert_down,
    cache_keys,
    cache_values,
    block_table,
    prefix_lengths,
    prompt_lengths,
    routed_experts,
):
    col_count = lax.axis_size("col")
    row_devices = lax.axis_size("row")
    col_index = lax.axis_index("col")
    row_index = lax.axis_index("row")
    tok_rows = hidden_in.shape[0]
    feature_width = hidden_in.shape[1]
    head_total = out_weight.shape[0]
    head_count = head_total // HEAD_DIM
    key_share = tok_rows // col_count
    request, position = token_layout(prompt_lengths[0], prefix_lengths[0], tok_rows)
    own_start = col_index * key_share
    key_position = lax.dynamic_slice_in_dim(position, own_start, key_share)
    key_request = lax.dynamic_slice_in_dim(request, own_start, key_share)
    residual = hidden_in.astype(jnp.float32)
    squares = lax.psum(jnp.sum(residual * residual, axis=1), "col")
    scale_one = lax.rsqrt(squares / D + norm_epsilon)
    normed = (residual * scale_one[:, None] * attn_gain[None, :]).astype(jnp.bfloat16)
    query_part = jnp.dot(normed, qkv_weight[:, :head_total], preferred_element_type=jnp.float32)
    query_sum = lax.psum(query_part, "col")
    queries = (rotate(query_sum, position, HEAD_DIM) * HEAD_DIM ** (-0.5)).astype(jnp.bfloat16)
    key_value = lax.psum_scatter(
        jnp.dot(normed, qkv_weight[:, head_total:], preferred_element_type=jnp.float32).astype(
            jnp.bfloat16
        ),
        "col",
        scatter_dimension=0,
        tiled=True,
    ).astype(jnp.float32)
    new_keys = rotate(key_value[:, :head_total], key_position, HEAD_DIM).astype(jnp.bfloat16)
    new_values = key_value[:, head_total:].astype(jnp.bfloat16)
    pool_size = cache_keys.shape[0]
    page_size = cache_keys.shape[1]
    req_count = block_table.shape[1]
    pages_each = block_table.shape[2] // col_count
    page_table = block_table[0].reshape(req_count, pages_each, col_count)
    own_pages = lax.dynamic_slice_in_dim(page_table, col_index, 1, 2).reshape(
        req_count * pages_each
    )
    pool_offset_begin = (row_index * col_count + col_index) * pool_size
    slot_ids = jnp.arange(pool_size, dtype=jnp.int32)
    entry_ids = jnp.arange(req_count * pages_each, dtype=jnp.int32)
    slot_match = (own_pages - pool_offset_begin)[None, :] == slot_ids[:, None]
    entry_request = entry_ids // pages_each
    entry_page = entry_ids % pages_each * col_count + col_index
    slot_request = jnp.sum(
        jnp.where(slot_match, entry_request[None, :], 0), axis=1, dtype=jnp.int32
    )
    slot_page = jnp.sum(jnp.where(slot_match, entry_page[None, :], 0), axis=1, dtype=jnp.int32)
    prefix_row = prefix_lengths[0]
    slot_prefix = jnp.sum(
        jnp.where(
            slot_request[:, None] == jnp.arange(req_count, dtype=jnp.int32)[None, :],
            prefix_row[None, :],
            0,
        ),
        axis=1,
        dtype=jnp.int32,
    )
    cache_position = (
        slot_page[:, None] * page_size + jnp.arange(page_size, dtype=jnp.int32)[None, :]
    )
    cache_live = (
        (cache_position < slot_prefix[:, None]).astype(jnp.int32).reshape(pool_size * page_size)
    )
    cache_request = jnp.broadcast_to(slot_request[:, None], (pool_size, page_size)).reshape(
        pool_size * page_size
    )
    cache_mask = (request[:, None] == cache_request[None, :]) & (cache_live[None, :] > 0)
    fresh_mask = (request[:, None] == key_request[None, :]) & (
        key_position[None, :] <= position[:, None]
    )
    group_size = math.gcd(head_count, 4)
    group_count = head_count // group_size
    query_heads = queries.reshape(tok_rows, head_count, HEAD_DIM)
    cached_key_heads = cache_keys.reshape(pool_size * page_size, head_count, HEAD_DIM)
    cached_value_heads = cache_values.reshape(pool_size * page_size, head_count, HEAD_DIM)
    fresh_key_heads = new_keys.reshape(key_share, head_count, HEAD_DIM)
    fresh_value_heads = new_values.reshape(key_share, head_count, HEAD_DIM)

    def head_group(group_index):
        first_head = group_index * group_size
        query_piece = lax.dynamic_slice_in_dim(query_heads, first_head, group_size, 1)
        key_piece = lax.dynamic_slice_in_dim(cached_key_heads, first_head, group_size, 1)
        value_piece = lax.dynamic_slice_in_dim(cached_value_heads, first_head, group_size, 1)
        fresh_key_piece = lax.dynamic_slice_in_dim(fresh_key_heads, first_head, group_size, 1)
        fresh_value_piece = lax.dynamic_slice_in_dim(fresh_value_heads, first_head, group_size, 1)
        score_matrix = jnp.einsum(
            "thd,khd->htk", query_piece, key_piece, preferred_element_type=jnp.float32
        )
        score_matrix = jnp.where(cache_mask[None], score_matrix, masked_score)
        fresh_scores = jnp.einsum(
            "thd,khd->htk", query_piece, fresh_key_piece, preferred_element_type=jnp.float32
        )
        fresh_scores = jnp.where(fresh_mask[None], fresh_scores, masked_score)
        largest = jnp.maximum(jnp.max(score_matrix, axis=2), jnp.max(fresh_scores, axis=2))
        cached_exp = jnp.where(cache_mask[None], jnp.exp(score_matrix - largest[:, :, None]), 0.0)
        fresh_exp = jnp.where(fresh_mask[None], jnp.exp(fresh_scores - largest[:, :, None]), 0.0)
        total_weight = jnp.sum(cached_exp, axis=2) + jnp.sum(fresh_exp, axis=2)
        summed = jnp.einsum(
            "htk,khd->thd",
            cached_exp.astype(jnp.bfloat16),
            value_piece,
            preferred_element_type=jnp.float32,
        )
        summed = summed + jnp.einsum(
            "htk,khd->thd",
            fresh_exp.astype(jnp.bfloat16),
            fresh_value_piece,
            preferred_element_type=jnp.float32,
        )
        return (largest, total_weight, summed.reshape(tok_rows, group_size * HEAD_DIM))

    largest, total_weight, summed = lax.map(head_group, jnp.arange(group_count, dtype=jnp.int32))
    largest, total_weight, summed = merged((largest, total_weight, summed), "col", combine_parts)
    attended = divide_rows(summed, total_weight).astype(jnp.bfloat16)
    projected = jnp.einsum(
        "gtx,gxo->to",
        attended,
        out_weight.reshape(group_count, group_size * HEAD_DIM, feature_width),
        preferred_element_type=jnp.float32,
    )
    attn_out = projected.astype(jnp.bfloat16)
    middle = (residual + residual_scale * attn_out.astype(jnp.float32)).astype(jnp.bfloat16)
    middle_wide = middle.astype(jnp.float32)
    squares_two = lax.psum(jnp.sum(middle_wide * middle_wide, axis=1), "col")
    scale_two = lax.rsqrt(squares_two / D + norm_epsilon)
    moe_normed_f = middle_wide * scale_two[:, None] * moe_gain[None, :]
    logits = lax.psum(jnp.dot(moe_normed_f, router_weight, precision=lax.Precision.HIGHEST), "col")
    moe_normed = moe_normed_f.astype(jnp.bfloat16)
    expert_local = expert_gate.shape[0]
    expert_total = expert_local * row_devices
    capacity = 2 * TOP * tok_rows // expert_total
    onehot_three = (
        routed_experts[:, :, None] == jnp.arange(expert_total, dtype=jnp.int32)[None, None, :]
    )
    selected_logits = jnp.sum(jnp.where(onehot_three, logits[:, None, :], 0.0), axis=2)
    first_gate = jax.nn.sigmoid(selected_logits[:, 0] - selected_logits[:, 1])
    gate_pair = jnp.stack([first_gate, 1.0 - first_gate], axis=1)
    onehot = onehot_three.astype(jnp.int32).reshape(tok_rows * TOP, expert_total)
    earlier = jnp.cumsum(onehot, axis=0, dtype=jnp.int32) - onehot
    slot_index = jnp.sum(earlier * onehot, axis=1, dtype=jnp.int32)
    target = routed_experts.reshape(tok_rows * TOP) * capacity + slot_index
    token_local = jnp.arange(tok_rows * TOP, dtype=jnp.int32) // TOP
    source = jnp.zeros((expert_total * capacity,), jnp.int32).at[target].set(token_local)
    filled = jnp.zeros((expert_total * capacity,), jnp.int32).at[target].set(1)
    outgoing = jnp.where(
        filled[:, None] > 0, moe_normed[source], jnp.zeros((), jnp.bfloat16)
    ).reshape(expert_total, capacity, feature_width)
    arrived = lax.all_to_all(outgoing, "row", split_axis=0, concat_axis=0, tiled=True)
    expert_rows = (
        arrived.reshape(row_devices, expert_local, capacity, feature_width)
        .transpose(1, 0, 2, 3)
        .reshape(expert_local, row_devices * capacity, feature_width)
    )
    feature_piece = lax.all_gather(expert_rows, "col", axis=2, tiled=True)
    gate_next = jnp.einsum(
        "erd,edf->erf", feature_piece, expert_gate, preferred_element_type=jnp.float32
    )
    up_next = jnp.einsum(
        "erd,edf->erf", feature_piece, expert_up, preferred_element_type=jnp.float32
    )
    hidden = (jax.nn.silu(gate_next) * up_next).astype(jnp.bfloat16)
    received_rows = hidden.shape[1]
    value_partial_sum = jnp.einsum(
        "efo,erf->oer", expert_down, hidden, preferred_element_type=jnp.float32
    )
    expert_out = lax.psum_scatter(
        value_partial_sum.reshape(
            lax.axis_size("col") * feature_width, expert_local * received_rows
        ).astype(jnp.bfloat16),
        "col",
        scatter_dimension=0,
        tiled=True,
    )
    returned = lax.all_to_all(
        expert_out.reshape(feature_width, expert_local, received_rows),
        "row",
        split_axis=2,
        concat_axis=1,
        tiled=True,
    )
    flat_back = returned.reshape(feature_width, expert_total * capacity)
    picked = (
        jnp.take(flat_back, target, axis=1)
        .astype(jnp.float32)
        .reshape(feature_width, tok_rows, TOP)
    )
    moe_columns = jnp.sum(picked * gate_pair[None, :, :], axis=2).astype(jnp.bfloat16)
    moe_out = moe_columns.T
    layer_out = (middle_wide + residual_scale * moe_out.astype(jnp.float32)).astype(jnp.bfloat16)
    return (attn_out, moe_out, layer_out)


def solution(mesh):
    in_specs = (
        P("row", "col"),
        P("col"),
        P("col", None),
        P(None, "col"),
        P("col"),
        P("col", None),
        P("row", None, "col"),
        P("row", None, "col"),
        P("row", "col", None),
        P(("row", "col"), None, None),
        P(("row", "col"), None, None),
        P("row", None, None),
        P("row", None),
        P("row", None),
        P("row", None),
    )
    out_specs = (P("row", "col"), P("row", "col"), P("row", "col"))
    return jax.shard_map(
        on_device, mesh=mesh, in_specs=in_specs, out_specs=out_specs, check_vma=False
    )
```

profile of v0, /device:TPU:2, one launch (start us, length us, event | category | flops | bytes accessed | tf_op | source)
XLA Modules:
  0.0 942.3 jit_solution(6926186442801343392)
XLA Ops:
  8.0 62.3 %psum.28 = f32[128]{0:T(128)S(1)} all-reduce(f32[128]{0:T(128)S(1)} %fusion.64), channel_id=1, replica_groups=mesh['row'=8,'col'=32] {'col'}, use_global_device_ids=true, to_apply=%region_1.2 | all-reduce | flops 128 | bytes 1024 | tf_op jit(solution)/shard_map/psum | solution.py:117
  70.3 2.7 convolution_convert_fusion
  77.7 5.0 reshape.454
  82.7 6.9 copy.162
  89.5 5.0 reshape.455
  94.5 6.7 copy.163
  102.5 88.4 %all-reduce.6.cloned.1.call-done = bf16[128,4608]{1,0:T(8,128)(2,1)} async-done(((bf16[128,4608]{1,0:T(8,128)(2,1)}), bf16[128,4608]{1,0:T(8,128)(2,1)}) %all-reduce.6.cloned.1.call-update) | async-done | bytes 1179664
  192.2 117.1 %all-reduce.4.cloned.1.call-done = f32[128,36,64]{0,2,1:T(8,128)} async-done(((f32[128,36,64]{0,2,1:T(8,128)}), f32[128,36,64]{0,2,1:T(8,128)}) %all-reduce.4.cloned.1.call-update) | async-done | bytes 1179664 | tf_op jit(solution)/shard_map/psum | solution.py:121
  310.9 51.9 %while.31 = (s32[]{:T(128)}, f32[9,4,128]{2,1,0:T(4,128)S(1)}, f32[9,4,128]{2,1,0:T(4,128)S(1)}, f32[9,128,256]{2,1,0:T(8,128)}, s32[9]{0:T(128)S(1)}, /*index=5...) while((s32[]{:T(128)}, f32[9,4,128]{2,1,0:T(4,128)S(1)}, ...), condition=%wide.region_16.17_spmd.clone.clone, body=%wide.region_11.16_spmd.clone.clone.sunk | while | flops 69911040 | bytes 5058339 | solution.py:215
  368.0 24.4 %all-gather = f32[288,4,128]{2,1,0:T(4,128)S(1)} all-gather(f32[9,4,128]{2,1,0:T(4,128)S(1)} %get-tuple-element.105), channel_id=2, replica_groups=mesh['row'=8,'col'=32] {'col'}, dimensions={0}, use_global_device_ids=true | all-gather | bytes 608256 | tf_op jit(solution)/shard_map/all_gather | solution.py:20
  392.5 25.6 %all-gather.1 = f32[288,4,128]{2,1,0:T(4,128)S(1)} all-gather(f32[9,4,128]{2,1,0:T(4,128)S(1)} %get-tuple-element.106), channel_id=3, replica_groups=mesh['row'=8,'col'=32] {'col'}, dimensions={0}, use_global_device_ids=true | all-gather | bytes 608256 | tf_op jit(solution)/shard_map/all_gather | solution.py:20
  418.2 76.0 %all-gather.8.cloned.1.call-done = f32[288,128,256]{2,1,0:T(8,128)} async-done(((f32[9,128,256]{2,1,0:T(8,128)}), f32[288,128,256]{2,1,0:T(8,128)}) %all-gather.8.cloned.1.call-update) | async-done | bytes 37748752 | tf_op jit(solution)/shard_map/all_gather | solution.py:20
  496.8 26.9 %slice.93 = f32[279,128,256]{2,1,0:T(8,128)} slice(f32[288,128,256]{2,1,0:T(8,128)} %all-gather.8.cloned.1.call-done), slice={[9:288], [0:128], [0:256]} | slice | bytes 73138176 | tf_op jit(solution)/shard_map/slice | solution.py:22
  523.7 168.2 %while.30 = (s32[]{:T(128)}, f32[9,4,128]{2,1,0:T(4,128)S(1)}, f32[9,4,128]{2,1,0:T(4,128)S(1)}, f32[9,128,256]{1,2,0:T(8,128)}, f32[31,9,4,128]{3,2,1,0:T(4,128...) while((s32[]{:T(128)}, f32[9,4,128]{2,1,0:T(4,128)S(1)}, ...), condition=%wide.region_18.19_spmd, body=%wide.region_17.18_spmd.sunk | while | flops 916994 | bytes 17676496 | solution.py:23
  531.9 2.6 fusion.111
  694.2 60.6 %psum.30 = f32[128]{0:T(128)S(1)} all-reduce(f32[128]{0:T(128)S(1)} %get-tuple-element.401), channel_id=1, replica_groups=mesh['row'=8,'col'=32] {'col'}, use_global_device_ids=true, to_apply=%region_24.25 | all-reduce | flops 128 | bytes 1024 | tf_op jit(solution)/shard_map/psum | solution.py:227
  756.5 15.9 %all_to_all.14 = bf16[8,64,72]{2,1,0:T(8,128)(2,1)S(1)} all-to-all(bf16[8,64,72]{2,1,0:T(8,128)(2,1)S(1)} %broadcast_select_fusion), channel_id=1, replica_groups=mesh['row'=8,'col'=32] {'row'}, dimensions={0} | all-to-all | bytes 147456 | tf_op jit(solution)/shard_map/all_to_all | solution.py:251
  773.2 44.9 %all-gather.6.cloned.1.call-done = bf16[1,512,2304]{1,2,0:T(8,128)(2,1)} async-done(((bf16[1,512,72]{1,2,0:T(8,128)(2,1)}), bf16[1,512,2304]{1,2,0:T(8,128)(2,1)}) %all-gather.6.cloned.1.call-update) | async-done | bytes 2359312 | tf_op jit(solution)/shard_map/all_gather | solution.py:257
  818.1 3.0 fusion.36
  821.2 3.4 fusion.33
  827.9 60.4 %psum.31 = f32[128,8]{0,1:T(8,128)S(1)} all-reduce(f32[128,8]{0,1:T(8,128)S(1)} %fusion.70), channel_id=1, replica_groups=mesh['row'=8,'col'=32] {'col'}, use_global_device_ids=true, to_apply=%region_27.28 | all-reduce | flops 1024 | bytes 8192 | tf_op jit(solution)/shard_map/psum | solution.py:230
  888.4 25.3 %reduce-scatter.4.cloned.1.call-done = bf16[72,512]{1,0:T(8,128)(2,1)} async-done(((bf16[2304,512]{1,0:T(8,128)(2,1)}), bf16[72,512]{1,0:T(8,128)(2,1)}) %reduce-scatter.4.cloned.1.call-update) | async-done | bytes 73744
  917.8 7.0 all-to-all-start.1
  925.0 8.3 all-to-all-done.1
  (695 shorter events, 240.1 us)
Async XLA Ops:
  7.2 814.0 %copy-start = (bf16[1,180,2304]{2,1,0:T(8,128)(2,1)S(1)}, bf16[1,180,2304]{2,1,0:T(8,128)(2,1)}, u32[]{:S(2)}) copy-start(bf16[1,180,2304]{2,1,0:T(8,128)(2,1)} %param.27) | copy-start | bytes 2488324
  7.2 183.7 %all-reduce.6.cloned.1.call-start = ((), (), s32[]{:S(2)}) async-start(), calls=%async_computation.7 | async-start | bytes 2359296
  70.3 2.9 copy-start.8
  70.3 2.9 copy-start.12
  73.1 2.9 copy-start.17
  73.1 3.2 copy-start.14
  73.1 3.4 copy-start.11
  73.1 4.6 copy-start.1
  73.1 236.2 %all-reduce.4.cloned.1.call-start = ((), (), s32[]{:S(2)}) async-start(), calls=%async_computation.3 | async-start | bytes 2359296 | tf_op jit(solution)/shard_map/psum | solution.py:121
  75.8 418.3 %all-gather.8.cloned.1.call-start = ((), (), s32[]{:S(2)}) async-start(), calls=%async_computation.5 | async-start | bytes 38928384 | tf_op jit(solution)/shard_map/all_gather | solution.py:20
  82.7 6.9 copy-start.2
  94.5 6.7 copy-start.18
  362.8 455.3 %all-gather.6.cloned.1.call-start = ((), (), s32[]{:S(2)}) async-start(), calls=%async_computation.4 | async-start | bytes 2433024 | tf_op jit(solution)/shard_map/all_gather | solution.py:257
  526.5 2.6 copy-start.4
  531.9 2.6 copy-start.4
  537.3 2.6 copy-start.4
  542.8 2.6 copy-start.4
  548.2 2.6 copy-start.4
  553.6 2.6 copy-start.4
  651.3 2.6 copy-start.4
  691.9 62.9 %copy-start.13 = (f32[72]{0:T(128)S(1)}, f32[72]{0:T(128)}, u32[]{:S(2)}) copy-start(f32[72]{0:T(128)} %param.23) | copy-start | bytes 868
  694.2 123.9 %copy-start.15 = (bf16[1,2304,180]{1,2,0:T(8,128)(2,1)S(1)}, bf16[1,2304,180]{1,2,0:T(8,128)(2,1)}, u32[]{:S(2)}) copy-start(bf16[1,2304,180]{1,2,0:T(8,128)(2,1)} %param.25) | copy-start | bytes 2488324
  773.1 140.5 %reduce-scatter.4.cloned.1.call-start = ((), (), s32[]{:S(2)}) async-start(), calls=%async_computation.6 | async-start | bytes 2433024
  917.8 15.5 %all-to-all-start.1 = ((bf16[8,2,2304]{2,1,0:T(2,128)(2,1)}), bf16[8,2,2304]{2,1,0:T(2,128)(2,1)S(1)}, u32[]{:S(2)}, u32[]{:S(2)}) async-start(bf16[8,2,2304]{2,1,0:T(2,128)(2,1)} %reshape.465), calls=%async_computation.1 | async-start | bytes 147456 | tf_op jit(solution)/shard_map/all_to_all | solution.py:277
  (122 other events, 206.0 us)
Sparse Core Ops, SparseCore 0:
  73.2 117.6 all-reduce.5
  194.2 115.0 all-reduce.3
  362.9 131.1 all-gather.7
  773.3 44.8 all-gather.5
  827.2 86.4 reduce-scatter.3
where the time goes:
time: 946 us; the launch traced here: 942 us
  waiting for transfers between devices  360 us (38%)
  blocking collectives  249 us (26%)
  local copies, waits for them, and re-layouts  164 us (17%)
  other arithmetic  97.8 us (10%)
  matrix products  40.8 us (4%)
  between operations  14.9 us (2%)
    psum x1, waiting for transfers between devices, on_device(): query_sum = lax.psum(query_part, 'col')  117 us
    unnamed x7, waiting for transfers between devices  114 us
    add x31, other arithmetic, combine_parts(): rescale(earlier_part[2], factor_one) + rescale(later_part[2], factor_two)  81.3 us
    all_gather x1, waiting for transfers between devices, merged(): pieces = jax.tree.map(lambda part: lax.all_gather(part, axis), value)  76 us
    psum x1, blocking collectives, on_device(): squares = lax.psum(jnp.sum(residual * residual, axis=1), 'col')  62.3 us
    psum x1, blocking collectives, on_device(): squares_two = lax.psum(jnp.sum(middle_wide * middle_wide, axis=1), 'col')  60.6 us
    psum x1, blocking collectives, on_device(): lax.psum(jnp.dot(moe_normed_f, router_weight, precision=lax.Precision.HIG...  60.4 us
    dynamic_slice x62, local copies, waits for them, and re-layouts, merged(): lax.scan(lambda running, slab: (join(running, slab), None), head, tail)  53.9 us
  transfers between devices with their start and end apart: 6, of which 6 were waited for; matrix products, arithmetic and copies ran while one was open for 4% of the time, Pallas kernels for 0%

commit v1 on v0

--- a/solution.py
+++ b/solution.py
@@ -114,20 +114,26 @@
     key_position = lax.dynamic_slice_in_dim(position, own_start, key_share)
     key_request = lax.dynamic_slice_in_dim(request, own_start, key_share)
     residual = hidden_in.astype(jnp.float32)
-    squares = lax.psum(jnp.sum(residual * residual, axis=1), "col")
+    squares = jnp.sum(lax.all_gather(jnp.sum(residual * residual, axis=1), "col"), axis=0)
     scale_one = lax.rsqrt(squares / D + norm_epsilon)
     normed = (residual * scale_one[:, None] * attn_gain[None, :]).astype(jnp.bfloat16)
     query_part = jnp.dot(normed, qkv_weight[:, :head_total], preferred_element_type=jnp.float32)
     query_sum = lax.psum(query_part, "col")
     queries = (rotate(query_sum, position, HEAD_DIM) * HEAD_DIM ** (-0.5)).astype(jnp.bfloat16)
-    key_value = lax.psum_scatter(
-        jnp.dot(normed, qkv_weight[:, head_total:], preferred_element_type=jnp.float32).astype(
-            jnp.bfloat16
-        ),
-        "col",
-        scatter_dimension=0,
-        tiled=True,
-    ).astype(jnp.float32)
+    kv_part = jnp.dot(
+        normed, qkv_weight[:, head_total:], preferred_element_type=jnp.float32
+    ).astype(jnp.bfloat16)
+    kv_width = kv_part.shape[1]
+    key_value = (
+        lax.psum_scatter(
+            kv_part.reshape(col_count * 8, key_share * kv_width // 8),
+            "col",
+            scatter_dimension=0,
+            tiled=True,
+        )
+        .reshape(key_share, kv_width)
+        .astype(jnp.float32)
+    )
     new_keys = rotate(key_value[:, :head_total], key_position, HEAD_DIM).astype(jnp.bfloat16)
     new_values = key_value[:, head_total:].astype(jnp.bfloat16)
     pool_size = cache_keys.shape[0]
@@ -171,63 +177,58 @@
     fresh_mask = (request[:, None] == key_request[None, :]) & (
         key_position[None, :] <= position[:, None]
     )
-    group_size = math.gcd(head_count, 4)
-    group_count = head_count // group_size
     query_heads = queries.reshape(tok_rows, head_count, HEAD_DIM)
-    cached_key_heads = cache_keys.reshape(pool_size * page_size, head_count, HEAD_DIM)
-    cached_value_heads = cache_values.reshape(pool_size * page_size, head_count, HEAD_DIM)
-    fresh_key_heads = new_keys.reshape(key_share, head_count, HEAD_DIM)
-    fresh_value_heads = new_values.reshape(key_share, head_count, HEAD_DIM)
-
-    def head_group(group_index):
-        first_head = group_index * group_size
-        query_piece = lax.dynamic_slice_in_dim(query_heads, first_head, group_size, 1)
-        key_piece = lax.dynamic_slice_in_dim(cached_key_heads, first_head, group_size, 1)
-        value_piece = lax.dynamic_slice_in_dim(cached_value_heads, first_head, group_size, 1)
-        fresh_key_piece = lax.dynamic_slice_in_dim(fresh_key_heads, first_head, group_size, 1)
-        fresh_value_piece = lax.dynamic_slice_in_dim(fresh_value_heads, first_head, group_size, 1)
-        score_matrix = jnp.einsum(
-            "thd,khd->htk", query_piece, key_piece, preferred_element_type=jnp.float32
-        )
-        score_matrix = jnp.where(cache_mask[None], score_matrix, masked_score)
-        fresh_scores = jnp.einsum(
-            "thd,khd->htk", query_piece, fresh_key_piece, preferred_element_type=jnp.float32
-        )
-        fresh_scores = jnp.where(fresh_mask[None], fresh_scores, masked_score)
-        largest = jnp.maximum(jnp.max(score_matrix, axis=2), jnp.max(fresh_scores, axis=2))
-        cached_exp = jnp.where(cache_mask[None], jnp.exp(score_matrix - largest[:, :, None]), 0.0)
-        fresh_exp = jnp.where(fresh_mask[None], jnp.exp(fresh_scores - largest[:, :, None]), 0.0)
-        total_weight = jnp.sum(cached_exp, axis=2) + jnp.sum(fresh_exp, axis=2)
-        summed = jnp.einsum(
-            "htk,khd->thd",
-            cached_exp.astype(jnp.bfloat16),
-            value_piece,
-            preferred_element_type=jnp.float32,
-        )
-        summed = summed + jnp.einsum(
-            "htk,khd->thd",
-            fresh_exp.astype(jnp.bfloat16),
-            fresh_value_piece,
-            preferred_element_type=jnp.float32,
-        )
-        return (largest, total_weight, summed.reshape(tok_rows, group_size * HEAD_DIM))
-
-    largest, total_weight, summed = lax.map(head_group, jnp.arange(group_count, dtype=jnp.int32))
-    largest, total_weight, summed = merged((largest, total_weight, summed), "col", combine_parts)
-    attended = divide_rows(summed, total_weight).astype(jnp.bfloat16)
-    projected = jnp.einsum(
-        "gtx,gxo->to",
-        attended,
-        out_weight.reshape(group_count, group_size * HEAD_DIM, feature_width),
+    key_heads = jnp.concatenate(
+        [cache_keys.reshape(pool_size * page_size, head_total), new_keys], axis=0
+    ).reshape(pool_size * page_size + key_share, head_count, HEAD_DIM)
+    value_heads = jnp.concatenate(
+        [cache_values.reshape(pool_size * page_size, head_total), new_values], axis=0
+    ).reshape(pool_size * page_size + key_share, head_count, HEAD_DIM)
+    key_mask = jnp.concatenate([cache_mask, fresh_mask], axis=1)
+    score_matrix = jnp.einsum(
+        "thd,khd->htk", query_heads, key_heads, preferred_element_type=jnp.float32
+    )
+    score_matrix = jnp.where(key_mask[None], score_matrix, masked_score)
+    local_max = jnp.max(score_matrix, axis=2)
+    weights = jnp.where(key_mask[None], jnp.exp(score_matrix - local_max[:, :, None]), 0.0)
+    local_total = jnp.sum(weights, axis=2)
+    local_sum = jnp.einsum(
+        "htk,khd->thd",
+        weights.astype(jnp.bfloat16),
+        value_heads,
         preferred_element_type=jnp.float32,
     )
+    largest = jnp.max(lax.all_gather(local_max, "col"), axis=0)
+    factor = jnp.exp(local_max - largest)
+    scaled_sum = local_sum * jnp.transpose(factor)[:, :, None]
+    scaled_total = jnp.transpose(local_total * factor)
+    joined = lax.psum(
+        jnp.concatenate([scaled_sum.reshape(tok_rows, head_total), scaled_total], axis=1), "col"
+    )
+    summed = joined[:, :head_total].reshape(tok_rows, head_count, HEAD_DIM)
+    total_weight = joined[:, head_total:]
+    attended = (summed / total_weight[:, :, None]).reshape(tok_rows, head_total).astype(
+        jnp.bfloat16
+    )
+    projected = jnp.dot(attended, out_weight, preferred_element_type=jnp.float32)
     attn_out = projected.astype(jnp.bfloat16)
     middle = (residual + residual_scale * attn_out.astype(jnp.float32)).astype(jnp.bfloat16)
     middle_wide = middle.astype(jnp.float32)
-    squares_two = lax.psum(jnp.sum(middle_wide * middle_wide, axis=1), "col")
-    scale_two = lax.rsqrt(squares_two / D + norm_epsilon)
+    router_part = jnp.dot(
+        middle_wide * moe_gain[None, :], router_weight, precision=lax.Precision.HIGHEST
+    )
+    stats = jnp.sum(
+        lax.all_gather(
+            jnp.concatenate(
+                [jnp.sum(middle_wide * middle_wide, axis=1, keepdims=True), router_part], axis=1
+            ),
+            "col",
+        ),
+        axis=0,
+    )
+    scale_two = lax.rsqrt(stats[:, 0] / D + norm_epsilon)
     moe_normed_f = middle_wide * scale_two[:, None] * moe_gain[None, :]
-    logits = lax.psum(jnp.dot(moe_normed_f, router_weight, precision=lax.Precision.HIGHEST), "col")
+    logits = stats[:, 1:] * scale_two[:, None]
     moe_normed = moe_normed_f.astype(jnp.bfloat16)
     expert_local = expert_gate.shape[0]
     expert_total = expert_local * row_devices

time: 946 us -> 605 us (0.64)
  blocking collectives: 249 us -> 83.8 us
  local copies, waits for them, and re-layouts: 164 us -> 45.1 us
  other arithmetic: 97.8 us -> 13 us
  waiting for transfers between devices: 360 us -> 418 us
  matrix products: 40.8 us -> 22.1 us
    psum x3 -> x0, blocking collectives: 183 us -> none  [the longest x1 62.3 us: on_device(): squares = lax.psum(jnp.sum(residual * residual, axis=1), 'col')]
    psum x0 -> x1, waiting for transfers between devices: none -> 112 us  [on_device(): lax.psum(jnp.concatenate([scaled_sum.reshape(tok_rows, head_total), scale...]
    reduce_scatter x0 -> x1, waiting for transfers between devices: none -> 83.2 us  [on_device(): lax.psum_scatter(kv_part.reshape(col_count * 8, key_share * kv_width // 8...]
    add x31 -> x0, other arithmetic: 81.3 us -> none  [combine_parts(): rescale(earlier_part[2], factor_one) + rescale(later_part[2], factor_two)]
    all_gather x1 -> x0, waiting for transfers between devices: 76 us -> none  [merged(): pieces = jax.tree.map(lambda part: lax.all_gather(part, axis), value)]
    dynamic_slice x80 -> x0, local copies, waits for them, and re-layouts: 59.3 us -> none  [the longest x62 53.9 us: merged(): lax.scan(lambda running, slab: (join(running, slab), None), head, tail)]
    psum x1, waiting for transfers between devices: 117 us -> 84.2 us  [on_device(): query_sum = lax.psum(query_part, 'col')]
    while x280 -> x0, local copies, waits for them, and re-layouts: 30.3 us -> none
  transfers between devices with their start and end apart: 6 -> 6, of which waited for: 6 -> 6; matrix products, arithmetic and copies ran while one was open for 4% -> 6% of each run, Pallas kernels for 0% -> 0%
where the time goes in v1:
time: 605 us; the launch traced here: 604 us
  waiting for transfers between devices  418 us (69%)
  blocking collectives  83.8 us (14%)
  local copies, waits for them, and re-layouts  45.1 us (7%)
  matrix products  22.1 us (4%)
  between operations  14.3 us (2%)
  other arithmetic  13 us (2%)
  starting transfers between devices  7.43 us (1%)
    psum x1, waiting for transfers between devices, on_device(): lax.psum(jnp.concatenate([scaled_sum.reshape(tok_rows, head_total), scale...  112 us
    unnamed x6, waiting for transfers between devices  86.3 us
    psum x1, waiting for transfers between devices, on_device(): query_sum = lax.psum(query_part, 'col')  84.2 us
    reduce_scatter x1, waiting for transfers between devices, on_device(): lax.psum_scatter(kv_part.reshape(col_count * 8, key_share * kv_width // 8...  83.2 us
    all_gather x1, waiting for transfers between devices, on_device(): feature_piece = lax.all_gather(expert_rows, 'col', axis=2, tiled=True)  44.2 us
    all_gather x1, blocking collectives, on_device(): largest = jnp.max(lax.all_gather(local_max, 'col'), axis=0)  23.3 us
    all_gather x1, blocking collectives, on_device(): lax.all_gather(jnp.concatenate([jnp.sum(middle_wide * middle_wide, axis=1...  22.5 us
    all_gather x1, blocking collectives, on_device(): lax.all_gather(jnp.sum(residual * residual, axis=1), 'col')  21.5 us
  transfers between devices with their start and end apart: 6, of which 6 were waited for; matrix products, arithmetic and copies ran while one was open for 6% of the time, Pallas kernels for 0%

profile of v1, /device:TPU:2, one launch (start us, length us, event | category | flops | bytes accessed | tf_op | source)
XLA Modules:
  0.0 604.0 jit_solution(13281635883749812086)
XLA Ops:
  8.1 21.5 %all-gather.3 = f32[32,1,128]{2,1,0:T(1,128)S(1)} all-gather(f32[1,1,128]{2,1,0:T(1,128)S(1)} %bitcast.118), channel_id=2, replica_groups=mesh['row'=8,'col'=32] {'col'}, dimensions={0}, use_global_device_ids=true | all-gather | bytes 16896 | tf_op jit(solution)/shard_map/all_gather | solution.py:117
  29.7 2.4 fusion.54
  37.2 7.8 %reshape.414 = bf16[512,36,64]{2,1,0:T(8,128)(2,1)} reshape(bf16[8,64,2304]{2,1,0:T(8,128)(2,1)} %param.24) | data formatting | bytes 4718592 | tf_op jit(solution)/shard_map/concatenate | solution.py:181
  45.0 6.9 %copy.134 = bf16[512,36,64]{0,2,1:T(8,128)(2,1)} copy(bf16[512,36,64]{2,1,0:T(8,128)(2,1)} %reshape.414) | data formatting | bytes 4718592 | tf_op jit(solution)/shard_map/concatenate | solution.py:181
  51.8 5.0 reshape.413
  56.8 6.7 %copy.133 = bf16[512,36,64]{0,2,1:T(8,128)(2,1)} copy(bf16[512,36,64]{2,1,0:T(8,128)(2,1)} %reshape.413) | data formatting | bytes 4718592 | tf_op jit(solution)/shard_map/concatenate | solution.py:184
  64.3 84.2 %all-reduce.3.cloned.1.call-done = f32[128,36,64]{0,2,1:T(8,128)} async-done(((f32[128,36,64]{0,2,1:T(8,128)}), f32[128,36,64]{0,2,1:T(8,128)}) %all-reduce.3.cloned.1.call-update) | async-done | bytes 1179664 | tf_op jit(solution)/shard_map/psum | solution.py:121
  148.5 2.3 multiply_subtract_fusion
  150.8 83.2 %reduce-scatter.5.cloned.1.call-done = bf16[8,2304]{1,0:T(8,128)(2,1)} async-done(((bf16[256,2304]{1,0:T(8,128)(2,1)}), bf16[8,2304]{1,0:T(8,128)(2,1)}) %reduce-scatter.5.cloned.1.call-update) | async-done | bytes 36880 | tf_op jit(solution)/shard_map/reduce_scatter | solution.py:128
  235.8 4.6 select_reduce_fusion
  240.4 2.1 fusion
  242.5 1.6 copy-done.1
  244.1 23.3 %all-gather.4 = f32[32,36,128]{2,1,0:T(8,128)S(1)} all-gather(f32[1,36,128]{2,1,0:T(8,128)S(1)} %bitcast.110), channel_id=3, replica_groups=mesh['row'=8,'col'=32] {'col'}, dimensions={0}, use_global_device_ids=true | all-gather | bytes 608256 | tf_op jit(solution)/shard_map/all_gather | solution.py:201
  267.5 7.0 %fusion.27 = f32[128,36,64]{0,2,1:T(8,128)S(1)} fusion(f32[36,128,516]{1,2,0:T(8,128)} %copy-done.1, f32[36,128]{1,0:T(8,128)S(1)} %get-tuple-element.27, pred[128,516]{0,1:T(8,128)(4,1)S(1)} %pad_add_fusion, bf16[4,36,64]{0,2,1:T(8,128)(2,1)S(1)} %bitcast.106, bf16[512,36,64]{0,2,1:T(8,128)(2,1)} %copy.133, f32[128,36]{0,1:T(8,128)S(1)} %get-tuple-element.12), kind=kOutput, calls=%fused_computation.30 | convolution fusion | flops 318910464 | bytes 13171200 | tf_op jit(solution)/shard_map/htk,khd->thd/dot_general | solution.py:195
  278.7 112.2 %all-reduce.5.cloned.1.call-done = f32[128,2340]{0,1:T(8,128)} async-done(((f32[128,2340]{0,1:T(8,128)}), f32[128,2340]{0,1:T(8,128)}) %all-reduce.5.cloned.1.call-update) | async-done | bytes 1198096 | tf_op jit(solution)/shard_map/psum | solution.py:205
  394.1 22.5 %all-gather.2 = f32[4096,9]{0,1:T(8,128)S(1)} all-gather(f32[128,9]{0,1:T(8,128)S(1)} %pad_maximum_fusion.1), channel_id=4, replica_groups=mesh['row'=8,'col'=32] {'col'}, dimensions={0}, use_global_device_ids=true | all-gather | bytes 152064 | tf_op jit(solution)/shard_map/all_gather | solution.py:221
  418.3 16.4 %all_to_all.14 = bf16[8,64,72]{2,1,0:T(8,128)(2,1)S(1)} all-to-all(bf16[8,64,72]{2,1,0:T(8,128)(2,1)S(1)} %broadcast_select_fusion), channel_id=1, replica_groups=mesh['row'=8,'col'=32] {'row'}, dimensions={0} | all-to-all | bytes 147456 | tf_op jit(solution)/shard_map/all_to_all | solution.py:252
  435.7 44.2 %all-gather.7.cloned.1.call-done = bf16[1,512,2304]{1,2,0:T(8,128)(2,1)} async-done(((bf16[1,512,72]{1,2,0:T(8,128)(2,1)}), bf16[1,512,2304]{1,2,0:T(8,128)(2,1)}) %all-gather.7.cloned.1.call-update) | async-done | bytes 2359312 | tf_op jit(solution)/shard_map/all_gather | solution.py:258
  479.9 3.0 fusion.20
  483.0 3.4 fusion.8
  486.4 2.5 copy.137
  489.2 86.2 %reduce-scatter.7.cloned.1.call-done = bf16[72,512]{1,0:T(8,128)(2,1)} async-done(((bf16[2304,512]{1,0:T(8,128)(2,1)}), bf16[72,512]{1,0:T(8,128)(2,1)}) %reduce-scatter.7.cloned.1.call-update) | async-done | bytes 73744
  579.5 7.0 %all-to-all-start.1 = ((bf16[8,2,2304]{2,1,0:T(2,128)(2,1)}), bf16[8,2,2304]{2,1,0:T(2,128)(2,1)S(1)}, u32[]{:S(2)}, u32[]{:S(2)}) async-start(bf16[8,2,2304]{2,1,0:T(2,128)(2,1)} %reshape.423), calls=%async_computation.2 | async-start | bytes 147456 | tf_op jit(solution)/shard_map/all_to_all | solution.py:278
  586.7 8.3 %all-to-all-done.1 = bf16[8,2,2304]{2,1,0:T(2,128)(2,1)S(1)} async-done(((bf16[8,2,2304]{2,1,0:T(2,128)(2,1)}), bf16[8,2,2304]{2,1,0:T(2,128)(2,1)S(1)}, u32[]{:S(2)}, u32[]{:S(2)}) %all-to-all-start.1) | async-done | bytes 73760 | tf_op jit(solution)/shard_map/all_to_all | solution.py:278
  (136 shorter events, 25.4 us)
Async XLA Ops:
  7.2 475.8 %copy-start = (bf16[1,180,2304]{2,1,0:T(8,128)(2,1)S(1)}, bf16[1,180,2304]{2,1,0:T(8,128)(2,1)}, u32[]{:S(2)}) copy-start(bf16[1,180,2304]{2,1,0:T(8,128)(2,1)} %param.23) | copy-start | bytes 2488324
  7.2 25.1 %copy-start.5 = (bf16[128,72]{0,1:T(8,128)(2,1)S(1)}, bf16[128,72]{0,1:T(8,128)(2,1)}, u32[]{:S(2)}) copy-start(bf16[128,72]{0,1:T(8,128)(2,1)} %param.15) | copy-start | bytes 55300
  7.2 25.1 %copy-start.3 = (bf16[72,6912]{1,0:T(8,128)(2,1)S(1)}, bf16[72,6912]{1,0:T(8,128)(2,1)}, u32[]{:S(2)}) copy-start(bf16[72,6912]{1,0:T(8,128)(2,1)} %param.17) | copy-start | bytes 2985988
  7.2 25.1 %copy-start.10 = (f32[72]{0:T(128)S(1)}, f32[72]{0:T(128)}, u32[]{:S(2)}) copy-start(f32[72]{0:T(128)} %param.16) | copy-start | bytes 868
  7.2 141.3 %all-reduce.3.cloned.1.call-start = ((), (), s32[]{:S(2)}) async-start(), calls=%async_computation.5 | async-start | bytes 2359296 | tf_op jit(solution)/shard_map/psum | solution.py:121
  32.2 2.1 copy-start.7
  32.2 2.2 copy-start.15
  32.2 2.5 copy-start.9
  32.2 201.8 %reduce-scatter.5.cloned.1.call-start = ((), (), s32[]{:S(2)}) async-start(), calls=%async_computation.4 | async-start | bytes 1216512 | tf_op jit(solution)/shard_map/reduce_scatter | solution.py:128
  32.9 3.3 copy-start.12
  34.2 356.7 %all-reduce.5.cloned.1.call-start = ((), (), s32[]{:S(2)}) async-start(), calls=%async_computation.6 | async-start | bytes 2400256 | tf_op jit(solution)/shard_map/psum | solution.py:205
  37.2 7.8 %copy-start.8 = (s32[8,3]{0,1:T(4,128)}, s32[8,3]{0,1:T(4,128)S(1)}, u32[]{:S(2)}) copy-start(s32[8,3]{0,1:T(4,128)S(1)} %reduce-window.14) | copy-start | bytes 292
  45.0 6.9 %copy-start.2 = (bf16[8,64,2304]{2,1,0:T(8,128)(2,1)S(1)}, bf16[8,64,2304]{2,1,0:T(8,128)(2,1)}, u32[]{:S(2)}) copy-start(bf16[8,64,2304]{2,1,0:T(8,128)(2,1)} %param.25) | copy-start | bytes 7077892
  56.8 7.1 %slice-start = ((s32[8,3]{0,1:T(4,128)}), s32[8,2]{0,1:T(2,128)S(1)}, s32[]{:S(2)}) async-start(s32[8,3]{0,1:T(4,128)} %copy-done.8), calls=%async_computation.9 | async-start | bytes 2048 | tf_op jit(solution)/shard_map/slice.1
  240.4 3.7 copy-start.1
  274.5 118.4 %copy-start.4 = (bf16[2304,72]{0,1:T(8,128)(2,1)S(1)}, bf16[2304,72]{0,1:T(8,128)(2,1)}, u32[]{:S(2)}) copy-start(bf16[2304,72]{0,1:T(8,128)(2,1)} %param.18) | copy-start | bytes 995332
  275.7 118.2 %copy-start.11 = (f32[72]{0:T(128)S(1)}, f32[72]{0:T(128)}, u32[]{:S(2)}) copy-start(f32[72]{0:T(128)} %param.19) | copy-start | bytes 868
  275.7 118.2 %copy-start.14 = (f32[72,8]{0,1:T(8,128)S(1)}, f32[72,8]{0,1:T(8,128)}, u32[]{:S(2)}) copy-start(f32[72,8]{0,1:T(8,128)} %param.20) | copy-start | bytes 6916
  275.7 204.2 %all-gather.7.cloned.1.call-start = ((), (), s32[]{:S(2)}) async-start(), calls=%async_computation.7 | async-start | bytes 2433024 | tf_op jit(solution)/shard_map/all_gather | solution.py:258
  393.0 87.0 %copy-start.13 = (bf16[1,2304,180]{1,2,0:T(8,128)(2,1)S(1)}, bf16[1,2304,180]{1,2,0:T(8,128)(2,1)}, u32[]{:S(2)}) copy-start(bf16[1,2304,180]{1,2,0:T(8,128)(2,1)} %param.21) | copy-start | bytes 2488324
  435.5 140.0 %reduce-scatter.7.cloned.1.call-start = ((), (), s32[]{:S(2)}) async-start(), calls=%async_computation.8 | async-start | bytes 2433024
  579.5 15.5 %all-to-all-start.1 = ((bf16[8,2,2304]{2,1,0:T(2,128)(2,1)}), bf16[8,2,2304]{2,1,0:T(2,128)(2,1)S(1)}, u32[]{:S(2)}, u32[]{:S(2)}) async-start(bf16[8,2,2304]{2,1,0:T(2,128)(2,1)} %reshape.423), calls=%async_computation.2 | async-start | bytes 147456 | tf_op jit(solution)/shard_map/all_to_all | solution.py:278
  596.8 0.6 copy-start.6
Sparse Core Ops, SparseCore 0:
  32.3 116.1 all-reduce.2
  152.3 81.6 reduce-scatter.4
  275.8 114.9 all-reduce.4
  435.6 44.2 all-gather.6
  488.9 86.4 reduce-scatter.6

commit v2 on v1

--- a/solution.py
+++ b/solution.py
@@ -22,6 +22,59 @@
     tail = jax.tree.map(lambda part: part[1:], pieces)
     running, _ = lax.scan(lambda running, slab: (join(running, slab), None), head, tail)
     return running
+
+
+def partner_swap(value, axis, bit, count):
+    pairs = [(device, device ^ (1 << bit)) for device in range(count)]
+    return lax.ppermute(value, axis, pairs)
+
+
+def tree_scatter(chunks, axis, bits, join):
+    count = chunks.shape[0]
+    depth = count.bit_length() - 1
+    me = lax.axis_index(axis)
+    present = list(range(depth - 1, -1, -1))
+    buffer = chunks.reshape((2,) * depth + chunks.shape[1:])
+    for bit in bits:
+        place = present.index(bit)
+        mine = (me >> bit) & 1
+        low = lax.index_in_dim(buffer, 0, place, keepdims=False)
+        high = lax.index_in_dim(buffer, 1, place, keepdims=False)
+        keep = jnp.where(mine > 0, high, low)
+        send = jnp.where(mine > 0, low, high)
+        buffer = join(keep, partner_swap(send, axis, bit, count))
+        present.pop(place)
+    return buffer
+
+
+def tree_gather(piece, axis, bits, count):
+    me = lax.axis_index(axis)
+    present = []
+    buffer = piece
+    for bit in bits:
+        mine = (me >> bit) & 1
+        other = partner_swap(buffer, axis, bit, count)
+        low = jnp.where(mine > 0, other, buffer)
+        high = jnp.where(mine > 0, buffer, other)
+        buffer = jnp.stack([low, high], axis=0)
+        present.insert(0, bit)
+    order = sorted(range(len(present)), key=lambda place: -present[place])
+    buffer = jnp.transpose(buffer, order + list(range(len(present), buffer.ndim)))
+    return buffer.reshape((count,) + piece.shape)
+
+
+def add_wide(keep, other):
+    return keep.astype(jnp.float32) + other.astype(jnp.float32)
+
+
+def join_softmax(keep, other):
+    width = keep.shape[-1] - 2
+    largest = jnp.maximum(keep[..., width], other[..., width])
+    factor_keep = jnp.exp(keep[..., width] - largest)
+    factor_other = jnp.exp(other[..., width] - largest)
+    summed = keep[..., :width] * factor_keep[..., None] + other[..., :width] * factor_other[..., None]
+    total = keep[..., width + 1] * factor_keep + other[..., width + 1] * factor_other
+    return jnp.concatenate([summed, largest[..., None], total[..., None]], axis=-1)
 
 
 def rotate(values, positions, head_dim):
@@ -117,23 +170,23 @@
     squares = jnp.sum(lax.all_gather(jnp.sum(residual * residual, axis=1), "col"), axis=0)
     scale_one = lax.rsqrt(squares / D + norm_epsilon)
     normed = (residual * scale_one[:, None] * attn_gain[None, :]).astype(jnp.bfloat16)
+    scatter_bits = [0] + list(range(1, col_count.bit_length() - 1))
+    gather_bits = scatter_bits[::-1]
     query_part = jnp.dot(normed, qkv_weight[:, :head_total], preferred_element_type=jnp.float32)
-    query_sum = lax.psum(query_part, "col")
-    queries = (rotate(query_sum, position, HEAD_DIM) * HEAD_DIM ** (-0.5)).astype(jnp.bfloat16)
     kv_part = jnp.dot(
         normed, qkv_weight[:, head_total:], preferred_element_type=jnp.float32
     ).astype(jnp.bfloat16)
-    kv_width = kv_part.shape[1]
-    key_value = (
-        lax.psum_scatter(
-            kv_part.reshape(col_count * 8, key_share * kv_width // 8),
-            "col",
-            scatter_dimension=0,
-            tiled=True,
-        )
-        .reshape(key_share, kv_width)
-        .astype(jnp.float32)
-    )
+    both_part = jnp.concatenate([query_part, kv_part.astype(jnp.float32)], axis=1)
+    both_sum = tree_scatter(
+        both_part.reshape(col_count, key_share, both_part.shape[1]), "col", scatter_bits, add_wide
+    )
+    own_queries = (
+        rotate(both_sum[:, :head_total], key_position, HEAD_DIM) * HEAD_DIM ** (-0.5)
+    ).astype(jnp.bfloat16)
+    queries = tree_gather(own_queries, "col", gather_bits, col_count).reshape(
+        tok_rows, head_total
+    )
+    key_value = both_sum[:, head_total:]
     new_keys = rotate(key_value[:, :head_total], key_position, HEAD_DIM).astype(jnp.bfloat16)
     new_values = key_value[:, head_total:].astype(jnp.bfloat16)
     pool_size = cache_keys.shape[0]
@@ -198,17 +251,22 @@
         value_heads,
         preferred_element_type=jnp.float32,
     )
-    largest = jnp.max(lax.all_gather(local_max, "col"), axis=0)
-    factor = jnp.exp(local_max - largest)
-    scaled_sum = local_sum * jnp.transpose(factor)[:, :, None]
-    scaled_total = jnp.transpose(local_total * factor)
-    joined = lax.psum(
-        jnp.concatenate([scaled_sum.reshape(tok_rows, head_total), scaled_total], axis=1), "col"
-    )
-    summed = joined[:, :head_total].reshape(tok_rows, head_count, HEAD_DIM)
-    total_weight = joined[:, head_total:]
-    attended = (summed / total_weight[:, :, None]).reshape(tok_rows, head_total).astype(
-        jnp.bfloat16
+    packed = jnp.concatenate(
+        [
+            local_sum,
+            jnp.transpose(local_max)[:, :, None],
+            jnp.transpose(local_total)[:, :, None],
+        ],
+        axis=2,
+    )
+    merged_rows = tree_scatter(
+        packed.reshape((col_count, key_share) + packed.shape[1:]), "col", scatter_bits, join_softmax
+    )
+    own_attended = (
+        merged_rows[..., :HEAD_DIM] / merged_rows[..., HEAD_DIM + 1][..., None]
+    ).reshape(key_share, head_total).astype(jnp.bfloat16)
+    attended = tree_gather(own_attended, "col", gather_bits, col_count).reshape(
+        tok_rows, head_total
     )
     projected = jnp.dot(attended, out_weight, preferred_element_type=jnp.float32)
     attn_out = projected.astype(jnp.bfloat16)

time: 605 us -> 506 us (0.84)
  waiting for transfers between devices: 418 us -> 236 us
  starting transfers between devices: 7.43 us -> 46.8 us
  local copies, waits for them, and re-layouts: 45.1 us -> 83.4 us
  other arithmetic: 13 us -> 34.9 us
  blocking collectives: 83.8 us -> 62.6 us
    psum x2 -> x0, waiting for transfers between devices: 196 us -> none  [the longest x1 112 us: on_device(): lax.psum(jnp.concatenate([scaled_sum.reshape(tok_rows, head_total), scale...]
    ppermute x0 -> x20, waiting for transfers between devices: none -> 98.3 us  [partner_swap(): return lax.ppermute(value, axis, pairs)]
    reduce_scatter x1 -> x0, waiting for transfers between devices: 83.2 us -> none  [on_device(): lax.psum_scatter(kv_part.reshape(col_count * 8, key_share * kv_width // 8...]
    ppermute x0 -> x20, starting transfers between devices: none -> 39.7 us  [partner_swap(): return lax.ppermute(value, axis, pairs)]
    all_gather x1 -> x0, blocking collectives: 23.3 us -> none  [on_device(): largest = jnp.max(lax.all_gather(local_max, 'col'), axis=0)]
    unnamed x40 -> x57, local copies, waits for them, and re-layouts: 7.25 us -> 18.7 us
    add x0 -> x9, other arithmetic: none -> 9.17 us  [the longest x5 5.1 us: add_wide(): return keep.astype(jnp.float32) + other.astype(jnp.float32)]
    another operation x2 -> x4, local copies, waits for them, and re-layouts: 0.01 us -> 6.17 us  [the longest x1 5.09 us: tree_scatter(): buffer = chunks.reshape((2,) * depth + chunks.shape[1:])]
  transfers between devices with their start and end apart: 6 -> 23, of which waited for: 6 -> 22; matrix products, arithmetic and copies ran while one was open for 6% -> 7% of each run, Pallas kernels for 0% -> 0%
where the time goes in v2:
time: 506 us; the launch traced here: 503 us
  waiting for transfers between devices  236 us (47%)
  local copies, waits for them, and re-layouts  83.4 us (16%)
  blocking collectives  62.6 us (12%)
  starting transfers between devices  46.8 us (9%)
  other arithmetic  34.9 us (7%)
  matrix products  23.8 us (5%)
  between operations  15.1 us (3%)
    ppermute x20, waiting for transfers between devices, partner_swap(): return lax.ppermute(value, axis, pairs)  98.3 us
    unnamed x3, waiting for transfers between devices  86.2 us
    all_gather x1, waiting for transfers between devices, on_device(): feature_piece = lax.all_gather(expert_rows, 'col', axis=2, tiled=True)  43.3 us
    ppermute x20, starting transfers between devices, partner_swap(): return lax.ppermute(value, axis, pairs)  39.7 us
    all_gather x1, blocking collectives, on_device(): lax.all_gather(jnp.concatenate([jnp.sum(middle_wide * middle_wide, axis=1...  23.2 us
    all_gather x1, blocking collectives, on_device(): lax.all_gather(jnp.sum(residual * residual, axis=1), 'col')  21.5 us
    unnamed x57, local copies, waits for them, and re-layouts  18.7 us
    all_to_all x1, blocking collectives, on_device(): lax.all_to_all(outgoing, 'row', split_axis=0, concat_axis=0, tiled=True)  17.8 us
  transfers between devices with their start and end apart: 23, of which 22 were waited for; matrix products, arithmetic and copies ran while one was open for 7% of the time, Pallas kernels for 0%

profile of v2, /device:TPU:2, one launch (start us, length us, event | category | flops | bytes accessed | tf_op | source)
XLA Modules:
  0.0 502.6 jit_solution(2583682312877225337)
XLA Ops:
  8.0 21.5 %all-gather.2 = f32[32,1,128]{2,1,0:T(1,128)S(1)} all-gather(f32[1,1,128]{2,1,0:T(1,128)S(1)} %bitcast.237), channel_id=2, replica_groups=mesh['row'=8,'col'=32] {'col'}, dimensions={0}, use_global_device_ids=true | all-gather | bytes 16896 | tf_op jit(solution)/shard_map/all_gather | solution.py:170
  37.1 5.1 %reshape_reshape.7 = f32[2,2,2,2,2,4,6912]{6,5,4,3,2,1,0:T(4,128)} reshape(f32[128,6912]{1,0:T(8,128)} %pad_maximum_fusion.1) | data formatting | bytes 7077888 | tf_op jit(solution)/shard_map/reshape;reshape | solution.py:37
  56.0 20.6 %collective-permute-done.1 = f32[2,2,2,4,6912]{4,3,0,1,2:T(4,128)S(1)} collective-permute-done((f32[2,2,2,4,6912]{4,3,0,1,2:T(4,128)S(1)}, f32[2,2,2,4,6912]{4,3,0,1,2:T(4,128)S(1)}, u32[]{:S(2)}, u32[]{:S(2)}) %collective-permute-start.1) | collective-permute-done | bytes 884768 | tf_op jit(solution)/shard_map/ppermute | solution.py:29
  80.3 11.5 %collective-permute-done.2 = f32[2,2,4,6912]{3,2,0,1:T(4,128)S(1)} collective-permute-done((f32[2,2,4,6912]{3,2,0,1:T(4,128)S(1)}, f32[2,2,4,6912]{3,2,0,1:T(4,128)S(1)}, u32[]{:S(2)}, u32[]{:S(2)}) %collective-permute-start.2) | collective-permute-done | bytes 442400 | tf_op jit(solution)/shard_map/ppermute | solution.py:29
  93.4 4.7 collective-permute-done.3
  100.9 3.8 collective-permute-done.4
  119.5 12.8 %collective-permute-start.7 = (bf16[2,2,4,2304]{3,2,1,0:T(4,128)(2,1)S(1)}, bf16[2,2,4,2304]{3,2,1,0:T(4,128)(2,1)S(1)}, u32[]{:S(2)}, u32[]{:S(2)}) collective-permute-start(bf16[2,2,4,2304]{3,2,1,0:T(4,128)(2,1)S(1)} %pad_maximum_fusion.10), channel_id=1, source_target_pairs={{0,4},{1,5},{2,6},{3,7},{4,0},{5,1},{6,2},{7,3},{8,12},{9,13},{10,... | collective-permute-start | bytes 221192 | tf_op jit(solution)/shard_map/ppermute | solution.py:29
  133.7 7.8 %reshape.383 = bf16[512,36,64]{2,1,0:T(8,128)(2,1)} reshape(bf16[8,64,2304]{2,1,0:T(8,128)(2,1)} %param.24) | data formatting | bytes 4718592 | tf_op jit(solution)/shard_map/concatenate | solution.py:234
  141.5 6.8 %copy.606 = bf16[512,36,64]{0,2,1:T(8,128)(2,1)} copy(bf16[512,36,64]{2,1,0:T(8,128)(2,1)} %reshape.383) | data formatting | bytes 4718592 | tf_op jit(solution)/shard_map/concatenate | solution.py:234
  148.4 5.0 reshape.382
  153.4 6.7 %copy.605 = bf16[512,36,64]{0,2,1:T(8,128)(2,1)} copy(bf16[512,36,64]{2,1,0:T(8,128)(2,1)} %reshape.382) | data formatting | bytes 4718592 | tf_op jit(solution)/shard_map/concatenate | solution.py:237
  169.5 4.3 select_reduce_fusion
  178.1 7.6 %fusion.24 = f32[128,36,64]{0,2,1:T(8,128)} fusion(f32[36,128,516]{1,2,0:T(8,128)} %copy-done.3, f32[36,128]{1,0:T(8,128)S(1)} %get-tuple-element.78, pred[128,516]{0,1:T(8,128)(4,1)S(1)} %pad_add_fusion, bf16[4,36,64]{0,2,1:T(8,128)(2,1)} %bitcast.222, bf16[512,36,64]{0,2,1:T(8,128)(2,1)S(1)} %copy-done.6), kind=kOutput, calls=%fused_computation.39 | convolution fusion | flops 318615552 | bytes 13152768 | tf_op jit(solution)/shard_map/htk,khd->thd/dot_general | solution.py:248
  187.5 4.7 copy.570
  220.3 12.9 %collective-permute-done.11 = f32[2,2,2,4,36,66]{5,3,4,2,1,0:T(4,128)S(1)} collective-permute-done((f32[2,2,2,4,36,66]{5,3,4,2,1,0:T(4,128)S(1)}, f32[2,2,2,4,36,66]{5,3,4,2,1,0:T(4,128)S(1)}, u32[]{:S(2)}, u32[]{:S(2)}) %collective-permute-start.11) | collective-permute-done | bytes 304160 | tf_op jit(solution)/shard_map/ppermute | solution.py:29
  242.1 7.8 %collective-permute-done.12 = f32[2,2,4,36,66]{4,2,3,1,0:T(4,128)S(1)} collective-permute-done((f32[2,2,4,36,66]{4,2,3,1,0:T(4,128)S(1)}, f32[2,2,4,36,66]{4,2,3,1,0:T(4,128)S(1)}, u32[]{:S(2)}, u32[]{:S(2)}) %collective-permute-start.12) | collective-permute-done | bytes 152096 | tf_op jit(solution)/shard_map/ppermute | solution.py:29
  252.7 5.6 %collective-permute-done.13 = f32[2,4,36,66]{2,1,3,0:T(4,128)S(1)} collective-permute-done((f32[2,4,36,66]{2,1,3,0:T(4,128)S(1)}, f32[2,4,36,66]{2,1,3,0:T(4,128)S(1)}, u32[]{:S(2)}, u32[]{:S(2)}) %collective-permute-start.13) | collective-permute-done | bytes 76064 | tf_op jit(solution)/shard_map/ppermute | solution.py:29
  261.2 4.0 collective-permute-done.14
  291.0 23.2 %all-gather.1 = f32[4096,9]{0,1:T(8,128)S(1)} all-gather(f32[128,9]{0,1:T(8,128)S(1)} %pad_maximum_fusion.14), channel_id=3, replica_groups=mesh['row'=8,'col'=32] {'col'}, dimensions={0}, use_global_device_ids=true | all-gather | bytes 152064 | tf_op jit(solution)/shard_map/all_gather | solution.py:279
  316.0 17.8 %all_to_all.14 = bf16[8,64,72]{2,1,0:T(8,128)(2,1)S(1)} all-to-all(bf16[8,64,72]{2,1,0:T(8,128)(2,1)S(1)} %broadcast_select_fusion), channel_id=1, replica_groups=mesh['row'=8,'col'=32] {'row'}, dimensions={0} | all-to-all | bytes 147456 | tf_op jit(solution)/shard_map/all_to_all | solution.py:310
  334.6 43.3 %all-gather.5.cloned.1.call-done = bf16[1,512,2304]{1,2,0:T(8,128)(2,1)} async-done(((bf16[1,512,72]{1,2,0:T(8,128)(2,1)}), bf16[1,512,2304]{1,2,0:T(8,128)(2,1)}) %all-gather.5.cloned.1.call-update) | async-done | bytes 2359312 | tf_op jit(solution)/shard_map/all_gather | solution.py:316
  387.5 86.1 %reduce-scatter.4.cloned.1.call-done = bf16[72,512]{1,0:T(8,128)(2,1)} async-done(((bf16[2304,512]{1,0:T(8,128)(2,1)}), bf16[72,512]{1,0:T(8,128)(2,1)}) %reduce-scatter.4.cloned.1.call-update) | async-done | bytes 73744
  477.7 7.0 %all-to-all-start.1 = ((bf16[8,2,2304]{2,1,0:T(2,128)(2,1)}), bf16[8,2,2304]{2,1,0:T(2,128)(2,1)S(1)}, u32[]{:S(2)}, u32[]{:S(2)}) async-start(bf16[8,2,2304]{2,1,0:T(2,128)(2,1)} %reshape.391), calls=%async_computation.1 | async-start | bytes 147456 | tf_op jit(solution)/shard_map/all_to_all | solution.py:336
  484.8 8.3 %all-to-all-done.1 = bf16[8,2,2304]{2,1,0:T(2,128)(2,1)S(1)} async-done(((bf16[8,2,2304]{2,1,0:T(2,128)(2,1)}), bf16[8,2,2304]{2,1,0:T(2,128)(2,1)S(1)}, u32[]{:S(2)}, u32[]{:S(2)}) %all-to-all-start.1) | async-done | bytes 73760 | tf_op jit(solution)/shard_map/all_to_all | solution.py:336
  (254 shorter events, 148.5 us)
Async XLA Ops:
  7.2 374.0 %copy-start = (bf16[1,180,2304]{2,1,0:T(8,128)(2,1)S(1)}, bf16[1,180,2304]{2,1,0:T(8,128)(2,1)}, u32[]{:S(2)}) copy-start(bf16[1,180,2304]{2,1,0:T(8,128)(2,1)} %param.23) | copy-start | bytes 2488324
  7.2 370.7 %all-gather.5.cloned.1.call-start = ((), (), s32[]{:S(2)}) async-start(), calls=%async_computation.3 | async-start | bytes 2433024 | tf_op jit(solution)/shard_map/all_gather | solution.py:316
  46.3 4.0 collective-permute-start
  54.6 22.0 %collective-permute-start.1 = (f32[2,2,2,4,6912]{4,3,0,1,2:T(4,128)S(1)}, f32[2,2,2,4,6912]{4,3,0,1,2:T(4,128)S(1)}, u32[]{:S(2)}, u32[]{:S(2)}) collective-permute-start(f32[2,2,2,4,6912]{4,3,0,1,2:T(4,128)S(1)} %select_bitcast_fusion.5), channel_id=1, source_target_pairs={{0,2},{1,3},{2,0},{3,1},{4,6},{5,7},{6,4},{7,5},{8,10},{9,11},{10,... | collective-permute-start | bytes 2654216 | tf_op jit(solution)/shard_map/ppermute | solution.py:29
  78.7 13.2 %collective-permute-start.2 = (f32[2,2,4,6912]{3,2,0,1:T(4,128)S(1)}, f32[2,2,4,6912]{3,2,0,1:T(4,128)S(1)}, u32[]{:S(2)}, u32[]{:S(2)}) collective-permute-start(f32[2,2,4,6912]{3,2,0,1:T(4,128)S(1)} %select_bitcast_fusion.8), channel_id=1, source_target_pairs={{0,4},{1,5},{2,6},{3,7},{4,0},{5,1},{6,2},{7,3},{8,12},{9,13},{10,... | collective-permute-start | bytes 1327112 | tf_op jit(solution)/shard_map/ppermute | solution.py:29
  92.1 6.1 %collective-permute-start.3 = (f32[2,4,6912]{2,1,0:T(4,128)S(1)}, f32[2,4,6912]{2,1,0:T(4,128)S(1)}, u32[]{:S(2)}, u32[]{:S(2)}) collective-permute-start(f32[2,4,6912]{2,1,0:T(4,128)S(1)} %select_bitcast_fusion.14), channel_id=1, source_target_pairs={{0,8},{1,9},{2,10},{3,11},{4,12},{5,13},{6,14},{7,15},{8,0},{9,1},... | collective-permute-start | bytes 663560 | tf_op jit(solution)/shard_map/ppermute | solution.py:29
  98.3 6.3 %collective-permute-start.4 = (f32[4,6912]{1,0:T(4,128)S(1)}, f32[4,6912]{1,0:T(4,128)S(1)}, u32[]{:S(2)}, u32[]{:S(2)}) collective-permute-start(f32[4,6912]{1,0:T(4,128)S(1)} %select_bitcast_fusion.21), channel_id=1, source_target_pairs={{0,16},{1,17},{2,18},{3,19},{4,20},{5,21},{6,22},{7,23},{8,24},{9,... | collective-permute-start | bytes 331784 | tf_op jit(solution)/shard_map/ppermute | solution.py:29
  110.0 5.4 %collective-permute-start.5 = (bf16[4,2304]{1,0:T(4,128)(2,1)S(1)}, bf16[4,2304]{1,0:T(4,128)(2,1)S(1)}, u32[]{:S(2)}, u32[]{:S(2)}) collective-permute-start(bf16[4,2304]{1,0:T(4,128)(2,1)S(1)} %convert_element_type.110), channel_id=1, source_target_pairs={{0,16},{1,17},{2,18},{3,19},{4,20},{5,21},{6,22},{7,23},{8,24},{9,... | collective-permute-start | bytes 55304 | tf_op jit(solution)/shard_map/ppermute | solution.py:29
  115.4 4.0 collective-permute-start.6
  119.5 40.6 %collective-permute-start.7 = (bf16[2,2,4,2304]{3,2,1,0:T(4,128)(2,1)S(1)}, bf16[2,2,4,2304]{3,2,1,0:T(4,128)(2,1)S(1)}, u32[]{:S(2)}, u32[]{:S(2)}) collective-permute-start(bf16[2,2,4,2304]{3,2,1,0:T(4,128)(2,1)S(1)} %pad_maximum_fusion.10), channel_id=1, source_target_pairs={{0,4},{1,5},{2,6},{3,7},{4,0},{5,1},{6,2},{7,3},{8,12},{9,13},{10,... | collective-permute-start | bytes 221192 | tf_op jit(solution)/shard_map/ppermute | solution.py:29
  160.3 5.2 %collective-permute-start.8 = (bf16[2,2,2,4,2304]{4,3,2,1,0:T(4,128)(2,1)S(1)}, bf16[2,2,2,4,2304]{4,3,2,1,0:T(4,128)(2,1)S(1)}, u32[]{:S(2)}, u32[]{:S(2)}) collective-permute-start(bf16[2,2,2,4,2304]{4,3,2,1,0:T(4,128)(2,1)S(1)} %pad_maximum_fusion.8), channel_id=1, source_target_pairs={{0,2},{1,3},{2,0},{3,1},{4,6},{5,7},{6,4},{7,5},{8,10},{9,11},{10,... | collective-permute-start | bytes 442376 | tf_op jit(solution)/shard_map/ppermute | solution.py:29
  165.9 1.7 collective-permute-start.9
  199.5 3.4 collective-permute-start.10
  217.8 15.5 %collective-permute-start.11 = (f32[2,2,2,4,36,66]{5,3,4,2,1,0:T(4,128)S(1)}, f32[2,2,2,4,36,66]{5,3,4,2,1,0:T(4,128)S(1)}, u32[]{:S(2)}, u32[]{:S(2)}) collective-permute-start(f32[2,2,2,4,36,66]{5,3,4,2,1,0:T(4,128)S(1)} %copy.577), channel_id=1, source_target_pairs={{0,2},{1,3},{2,0},{3,1},{4,6},{5,7},{6,4},{7,5},{8,10},{9,11},{10,... | collective-permute-start | bytes 912392 | tf_op jit(solution)/shard_map/ppermute | solution.py:29
  240.1 9.8 %collective-permute-start.12 = (f32[2,2,4,36,66]{4,2,3,1,0:T(4,128)S(1)}, f32[2,2,4,36,66]{4,2,3,1,0:T(4,128)S(1)}, u32[]{:S(2)}, u32[]{:S(2)}) collective-permute-start(f32[2,2,4,36,66]{4,2,3,1,0:T(4,128)S(1)} %copy.581), channel_id=1, source_target_pairs={{0,4},{1,5},{2,6},{3,7},{4,0},{5,1},{6,2},{7,3},{8,12},{9,13},{10,... | collective-permute-start | bytes 456200 | tf_op jit(solution)/shard_map/ppermute | solution.py:29
  251.4 6.9 %collective-permute-start.13 = (f32[2,4,36,66]{2,1,3,0:T(4,128)S(1)}, f32[2,4,36,66]{2,1,3,0:T(4,128)S(1)}, u32[]{:S(2)}, u32[]{:S(2)}) collective-permute-start(f32[2,4,36,66]{2,1,3,0:T(4,128)S(1)} %select_bitcast_fusion.13), channel_id=1, source_target_pairs={{0,8},{1,9},{2,10},{3,11},{4,12},{5,13},{6,14},{7,15},{8,0},{9,1},... | collective-permute-start | bytes 228104 | tf_op jit(solution)/shard_map/ppermute | solution.py:29
  258.6 6.6 %collective-permute-start.14 = (f32[4,36,66]{1,0,2:T(4,128)S(1)}, f32[4,36,66]{1,0,2:T(4,128)S(1)}, u32[]{:S(2)}, u32[]{:S(2)}) collective-permute-start(f32[4,36,66]{1,0,2:T(4,128)S(1)} %get-tuple-element.53), channel_id=1, source_target_pairs={{0,16},{1,17},{2,18},{3,19},{4,20},{5,21},{6,22},{7,23},{8,24},{9,... | collective-permute-start | bytes 114056 | tf_op jit(solution)/shard_map/ppermute | solution.py:29
  265.5 5.4 %collective-permute-start.15 = (bf16[4,2304]{1,0:T(4,128)(2,1)S(1)}, bf16[4,2304]{1,0:T(4,128)(2,1)S(1)}, u32[]{:S(2)}, u32[]{:S(2)}) collective-permute-start(bf16[4,2304]{1,0:T(4,128)(2,1)S(1)} %convert_element_type.113), channel_id=1, source_target_pairs={{0,16},{1,17},{2,18},{3,19},{4,20},{5,21},{6,22},{7,23},{8,24},{9,... | collective-permute-start | bytes 55304 | tf_op jit(solution)/shard_map/ppermute | solution.py:29
  270.9 4.0 collective-permute-start.16
  275.0 6.1 %collective-permute-start.17 = (bf16[2,2,4,2304]{3,2,1,0:T(4,128)(2,1)S(1)}, bf16[2,2,4,2304]{3,2,1,0:T(4,128)(2,1)S(1)}, u32[]{:S(2)}, u32[]{:S(2)}) collective-permute-start(bf16[2,2,4,2304]{3,2,1,0:T(4,128)(2,1)S(1)} %pad_maximum_fusion.11), channel_id=1, source_target_pairs={{0,4},{1,5},{2,6},{3,7},{4,0},{5,1},{6,2},{7,3},{8,12},{9,13},{10,... | collective-permute-start | bytes 221192 | tf_op jit(solution)/shard_map/ppermute | solution.py:29
  281.4 5.2 %collective-permute-start.18 = (bf16[2,2,2,4,2304]{4,3,2,1,0:T(4,128)(2,1)S(1)}, bf16[2,2,2,4,2304]{4,3,2,1,0:T(4,128)(2,1)S(1)}, u32[]{:S(2)}, u32[]{:S(2)}) collective-permute-start(bf16[2,2,2,4,2304]{4,3,2,1,0:T(4,128)(2,1)S(1)} %pad_maximum_fusion.9), channel_id=1, source_target_pairs={{0,2},{1,3},{2,0},{3,1},{4,6},{5,7},{6,4},{7,5},{8,10},{9,11},{10,... | collective-permute-start | bytes 442376 | tf_op jit(solution)/shard_map/ppermute | solution.py:29
  287.0 1.7 collective-permute-start.19
  334.6 139.0 %reduce-scatter.4.cloned.1.call-start = ((), (), s32[]{:S(2)}) async-start(), calls=%async_computation.4 | async-start | bytes 2433024
  477.7 15.5 %all-to-all-start.1 = ((bf16[8,2,2304]{2,1,0:T(2,128)(2,1)}), bf16[8,2,2304]{2,1,0:T(2,128)(2,1)S(1)}, u32[]{:S(2)}, u32[]{:S(2)}) async-start(bf16[8,2,2304]{2,1,0:T(2,128)(2,1)} %reshape.391), calls=%async_computation.1 | async-start | bytes 147456 | tf_op jit(solution)/shard_map/all_to_all | solution.py:336
  (19 other events, 66.7 us)
Sparse Core Ops, SparseCore 0:
  334.7 43.1 all-gather.4
  387.2 86.3 reduce-scatter.3

commit v3 on v2

--- a/solution.py
+++ b/solution.py
@@ -313,26 +313,31 @@
         .transpose(1, 0, 2, 3)
         .reshape(expert_local, row_devices * capacity, feature_width)
     )
-    feature_piece = lax.all_gather(expert_rows, "col", axis=2, tiled=True)
+    gathered = tree_gather(
+        jnp.transpose(expert_rows, (0, 2, 1)), "col", gather_bits, col_count
+    )
+    feature_piece = jnp.transpose(gathered, (1, 0, 2, 3)).reshape(
+        expert_local, col_count * feature_width, gathered.shape[3]
+    )
     gate_next = jnp.einsum(
-        "erd,edf->erf", feature_piece, expert_gate, preferred_element_type=jnp.float32
+        "edr,edf->erf", feature_piece, expert_gate, preferred_element_type=jnp.float32
     )
     up_next = jnp.einsum(
-        "erd,edf->erf", feature_piece, expert_up, preferred_element_type=jnp.float32
+        "edr,edf->erf", feature_piece, expert_up, preferred_element_type=jnp.float32
     )
     hidden = (jax.nn.silu(gate_next) * up_next).astype(jnp.bfloat16)
     received_rows = hidden.shape[1]
     value_partial_sum = jnp.einsum(
         "efo,erf->oer", expert_down, hidden, preferred_element_type=jnp.float32
     )
-    expert_out = lax.psum_scatter(
+    expert_out = tree_scatter(
         value_partial_sum.reshape(
-            lax.axis_size("col") * feature_width, expert_local * received_rows
+            col_count, feature_width, expert_local * received_rows
         ).astype(jnp.bfloat16),
         "col",
-        scatter_dimension=0,
-        tiled=True,
-    )
+        scatter_bits,
+        add_wide,
+    ).astype(jnp.bfloat16)
     returned = lax.all_to_all(
         expert_out.reshape(feature_width, expert_local, received_rows),
         "row",

time: 506 us -> 459 us (0.907)
  waiting for transfers between devices: 236 us -> 192 us
  between operations: 15.1 us -> 2.11 us
    unnamed x3 -> x0, waiting for transfers between devices: 86.2 us -> none
    ppermute x20 -> x30, waiting for transfers between devices: 98.3 us -> 183 us  [partner_swap(): return lax.ppermute(value, axis, pairs)]
    all_gather x1 -> x0, waiting for transfers between devices: 43.3 us -> none  [on_device(): feature_piece = lax.all_gather(expert_rows, 'col', axis=2, tiled=True)]
    ppermute x20 -> x30, starting transfers between devices: 39.7 us -> 47.8 us  [partner_swap(): return lax.ppermute(value, axis, pairs)]
  transfers between devices with their start and end apart: 23 -> 31, of which waited for: 22 -> 30; matrix products, arithmetic and copies ran while one was open for 7% -> 8% of each run, Pallas kernels for 0% -> 0%
where the time goes in v3:
time: 459 us; the launch traced here: 451 us
  waiting for transfers between devices  192 us (42%)
  local copies, waits for them, and re-layouts  83.2 us (18%)
  blocking collectives  62.5 us (14%)
  starting transfers between devices  51.1 us (11%)
  other arithmetic  37.5 us (8%)
  matrix products  22.7 us (5%)
    ppermute x30, waiting for transfers between devices, partner_swap(): return lax.ppermute(value, axis, pairs)  183 us
    ppermute x30, starting transfers between devices, partner_swap(): return lax.ppermute(value, axis, pairs)  47.8 us
    all_gather x1, blocking collectives, on_device(): lax.all_gather(jnp.concatenate([jnp.sum(middle_wide * middle_wide, axis=1...  23.2 us
    all_gather x1, blocking collectives, on_device(): lax.all_gather(jnp.sum(residual * residual, axis=1), 'col')  21.5 us
    all_to_all x1, blocking collectives, on_device(): lax.all_to_all(outgoing, 'row', split_axis=0, concat_axis=0, tiled=True)  17.8 us
    unnamed x57, local copies, waits for them, and re-layouts  16.1 us
    concatenate x2, local copies, waits for them, and re-layouts, on_device(): jnp.concatenate([cache_keys.reshape(pool_size * page_size, head_total), n...  14.7 us
    concatenate x2, local copies, waits for them, and re-layouts, on_device(): jnp.concatenate([cache_values.reshape(pool_size * page_size, head_total),...  11.7 us
  transfers between devices with their start and end apart: 31, of which 30 were waited for; matrix products, arithmetic and copies ran while one was open for 8% of the time, Pallas kernels for 0%

profile of v3, /device:TPU:2, one launch (start us, length us, event | category | flops | bytes accessed | tf_op | source)
XLA Modules:
  0.0 450.9 jit_solution(15995735033258782341)
XLA Ops:
  1.5 21.5 %all-gather.2 = f32[32,1,128]{2,1,0:T(1,128)S(1)} all-gather(f32[1,1,128]{2,1,0:T(1,128)S(1)} %bitcast.356), channel_id=2, replica_groups=mesh['row'=8,'col'=32] {'col'}, dimensions={0}, use_global_device_ids=true | all-gather | bytes 16896 | tf_op jit(solution)/shard_map/all_gather | solution.py:170
  30.5 5.1 %reshape_reshape.7 = f32[2,2,2,2,2,4,6912]{6,5,4,3,2,1,0:T(4,128)} reshape(f32[128,6912]{1,0:T(8,128)} %pad_maximum_fusion.1) | data formatting | bytes 7077888 | tf_op jit(solution)/shard_map/reshape;reshape | solution.py:37
  49.4 20.6 %collective-permute-done.1 = f32[2,2,2,4,6912]{4,3,0,1,2:T(4,128)S(1)} collective-permute-done((f32[2,2,2,4,6912]{4,3,0,1,2:T(4,128)S(1)}, f32[2,2,2,4,6912]{4,3,0,1,2:T(4,128)S(1)}, u32[]{:S(2)}, u32[]{:S(2)}) %collective-permute-start.1) | collective-permute-done | bytes 884768 | tf_op jit(solution)/shard_map/ppermute | solution.py:29
  73.7 11.5 %collective-permute-done.2 = f32[2,2,4,6912]{3,2,0,1:T(4,128)S(1)} collective-permute-done((f32[2,2,4,6912]{3,2,0,1:T(4,128)S(1)}, f32[2,2,4,6912]{3,2,0,1:T(4,128)S(1)}, u32[]{:S(2)}, u32[]{:S(2)}) %collective-permute-start.2) | collective-permute-done | bytes 442400 | tf_op jit(solution)/shard_map/ppermute | solution.py:29
  86.8 4.7 %collective-permute-done.3 = f32[2,4,6912]{2,1,0:T(4,128)S(1)} collective-permute-done((f32[2,4,6912]{2,1,0:T(4,128)S(1)}, f32[2,4,6912]{2,1,0:T(4,128)S(1)}, u32[]{:S(2)}, u32[]{:S(2)}) %collective-permute-start.3) | collective-permute-done | bytes 221216 | tf_op jit(solution)/shard_map/ppermute | solution.py:29
  116.2 7.8 %reshape.410 = bf16[512,36,64]{2,1,0:T(8,128)(2,1)} reshape(bf16[8,64,2304]{2,1,0:T(8,128)(2,1)} %param.24) | data formatting | bytes 4718592 | tf_op jit(solution)/shard_map/concatenate | solution.py:234
  124.1 6.8 %copy.783 = bf16[512,36,64]{0,2,1:T(8,128)(2,1)} copy(bf16[512,36,64]{2,1,0:T(8,128)(2,1)} %reshape.410) | data formatting | bytes 4718592 | tf_op jit(solution)/shard_map/concatenate | solution.py:234
  130.9 5.0 %reshape.409 = bf16[512,36,64]{2,1,0:T(8,128)(2,1)} reshape(bf16[8,64,2304]{2,1,0:T(8,128)(2,1)S(1)} %copy-done.5) | data formatting | bytes 4718592 | tf_op jit(solution)/shard_map/concatenate | solution.py:237
  135.9 6.7 %copy.782 = bf16[512,36,64]{0,2,1:T(8,128)(2,1)} copy(bf16[512,36,64]{2,1,0:T(8,128)(2,1)} %reshape.409) | data formatting | bytes 4718592 | tf_op jit(solution)/shard_map/concatenate | solution.py:237
  160.6 7.5 %fusion.20 = f32[128,36,64]{0,2,1:T(8,128)} fusion(f32[36,128,516]{1,2,0:T(8,128)} %copy-done.3, f32[36,128]{1,0:T(8,128)S(1)} %get-tuple-element.80, pred[128,516]{0,1:T(8,128)(4,1)S(1)} %pad_add_fusion, bf16[4,36,64]{0,2,1:T(8,128)(2,1)} %bitcast.341, bf16[512,36,64]{0,2,1:T(8,128)(2,1)S(1)} %copy-done.6), kind=kOutput, calls=%fused_computation.38 | convolution fusion | flops 318615552 | bytes 13152768 | tf_op jit(solution)/shard_map/htk,khd->thd/dot_general | solution.py:248
  170.0 4.7 %copy.722 = f32[2,2,2,2,2,4,36,64]{6,5,7,3,2,1,0,4:T(4,128)} copy(f32[2,2,2,2,2,4,36,64]{7,5,4,3,2,1,0,6:T(4,128)S(1)} %bitcast.329) | data formatting | bytes 2359296 | tf_op jit(solution)/shard_map/concatenate | solution.py:254
  182.0 8.7 %collective-permute-start.10 = (f32[2,2,2,2,4,36,66]{6,4,5,3,2,1,0:T(4,128)}, f32[2,2,2,2,4,36,66]{6,4,5,3,2,1,0:T(4,128)S(1)}, u32[]{:S(2)}, u32[]{:S(2)}) collective-permute-start(f32[2,2,2,2,4,36,66]{6,4,5,3,2,1,0:T(4,128)} %copy.725), channel_id=1, source_target_pairs={{0,1},{1,0},{2,3},{3,2},{4,5},{5,4},{6,7},{7,6},{8,9},{9,8},{10,11... | collective-permute-start | bytes 1824776 | tf_op jit(solution)/shard_map/ppermute | solution.py:29
  210.9 13.0 %collective-permute-done.11 = f32[2,2,2,4,36,66]{5,3,4,2,1,0:T(4,128)S(1)} collective-permute-done((f32[2,2,2,4,36,66]{5,3,4,2,1,0:T(4,128)S(1)}, f32[2,2,2,4,36,66]{5,3,4,2,1,0:T(4,128)S(1)}, u32[]{:S(2)}, u32[]{:S(2)}) %collective-permute-start.11) | collective-permute-done | bytes 304160 | tf_op jit(solution)/shard_map/ppermute | solution.py:29
  232.8 7.8 %collective-permute-done.12 = f32[2,2,4,36,66]{4,2,3,1,0:T(4,128)S(1)} collective-permute-done((f32[2,2,4,36,66]{4,2,3,1,0:T(4,128)S(1)}, f32[2,2,4,36,66]{4,2,3,1,0:T(4,128)S(1)}, u32[]{:S(2)}, u32[]{:S(2)}) %collective-permute-start.12) | collective-permute-done | bytes 152096 | tf_op jit(solution)/shard_map/ppermute | solution.py:29
  243.3 5.7 %collective-permute-done.13 = f32[2,4,36,66]{2,1,3,0:T(4,128)S(1)} collective-permute-done((f32[2,4,36,66]{2,1,3,0:T(4,128)S(1)}, f32[2,4,36,66]{2,1,3,0:T(4,128)S(1)}, u32[]{:S(2)}, u32[]{:S(2)}) %collective-permute-start.13) | collective-permute-done | bytes 76064 | tf_op jit(solution)/shard_map/ppermute | solution.py:29
  281.8 23.2 %all-gather.1 = f32[4096,9]{0,1:T(8,128)S(1)} all-gather(f32[128,9]{0,1:T(8,128)S(1)} %pad_maximum_fusion.18), channel_id=3, replica_groups=mesh['row'=8,'col'=32] {'col'}, dimensions={0}, use_global_device_ids=true | all-gather | bytes 152064 | tf_op jit(solution)/shard_map/all_gather | solution.py:279
  306.7 17.8 %all_to_all.14 = bf16[8,64,72]{2,1,0:T(8,128)(2,1)S(1)} all-to-all(bf16[8,64,72]{2,1,0:T(8,128)(2,1)S(1)} %broadcast_select_fusion), channel_id=1, replica_groups=mesh['row'=8,'col'=32] {'row'}, dimensions={0} | all-to-all | bytes 147456 | tf_op jit(solution)/shard_map/all_to_all | solution.py:310
  338.1 7.3 %collective-permute-done.22 = bf16[2,2,1,72,512]{4,3,2,1,0:T(8,128)(2,1)S(1)} collective-permute-done((bf16[2,2,1,72,512]{4,3,2,1,0:T(8,128)(2,1)S(1)}, bf16[2,2,1,72,512]{4,3,2,1,0:T(8,128)(2,1)S(1)}, u32[]{:S(2)}, u32[]{:S(2)}) %collective-permute-start.22) | collective-permute-done | bytes 294944 | tf_op jit(solution)/shard_map/ppermute | solution.py:29
  347.2 9.4 %collective-permute-done.23 = bf16[2,2,2,1,72,512]{5,4,3,2,1,0:T(8,128)(2,1)S(1)} collective-permute-done((bf16[2,2,2,1,72,512]{5,4,3,2,1,0:T(8,128)(2,1)S(1)}, bf16[2,2,2,1,72,512]{5,4,3,2,1,0:T(8,128)(2,1)S(1)}, u32[]{:S(2)}, u32[]{:S(2)}) %collective-permute-start.23) | collective-permute-done | bytes 589856 | tf_op jit(solution)/shard_map/ppermute | solution.py:29
  374.9 27.2 %collective-permute-done.26 = f32[2,2,2,72,512]{4,3,2,1,0:T(8,128)S(1)} collective-permute-done((f32[2,2,2,72,512]{4,3,2,1,0:T(8,128)S(1)}, f32[2,2,2,72,512]{4,3,2,1,0:T(8,128)S(1)}, u32[]{:S(2)}, u32[]{:S(2)}) %collective-permute-start.26) | collective-permute-done | bytes 1179680 | tf_op jit(solution)/shard_map/ppermute | solution.py:29
  404.3 14.4 %collective-permute-done.27 = f32[2,2,72,512]{3,2,1,0:T(8,128)S(1)} collective-permute-done((f32[2,2,72,512]{3,2,1,0:T(8,128)S(1)}, f32[2,2,72,512]{3,2,1,0:T(8,128)S(1)}, u32[]{:S(2)}, u32[]{:S(2)}) %collective-permute-start.27) | collective-permute-done | bytes 589856 | tf_op jit(solution)/shard_map/ppermute | solution.py:29
  419.4 7.0 %collective-permute-done.28 = f32[2,72,512]{2,1,0:T(8,128)S(1)} collective-permute-done((f32[2,72,512]{2,1,0:T(8,128)S(1)}, f32[2,72,512]{2,1,0:T(8,128)S(1)}, u32[]{:S(2)}, u32[]{:S(2)}) %collective-permute-start.28) | collective-permute-done | bytes 294944 | tf_op jit(solution)/shard_map/ppermute | solution.py:29
  428.0 5.2 %collective-permute-done.29 = f32[72,512]{1,0:T(8,128)S(1)} collective-permute-done((f32[72,512]{1,0:T(8,128)S(1)}, f32[72,512]{1,0:T(8,128)S(1)}, u32[]{:S(2)}, u32[]{:S(2)}) %collective-permute-start.29) | collective-permute-done | bytes 147488 | tf_op jit(solution)/shard_map/ppermute | solution.py:29
  439.7 8.2 %all-to-all-done.1 = bf16[8,2,2304]{2,1,0:T(2,128)(2,1)S(1)} async-done(((bf16[8,2,2304]{2,1,0:T(2,128)(2,1)}), bf16[8,2,2304]{2,1,0:T(2,128)(2,1)S(1)}, u32[]{:S(2)}, u32[]{:S(2)}) %all-to-all-start.1) | async-done | bytes 73760 | tf_op jit(solution)/shard_map/all_to_all | solution.py:341
  (294 shorter events, 192.0 us)
Async XLA Ops:
  48.0 22.0 %collective-permute-start.1 = (f32[2,2,2,4,6912]{4,3,0,1,2:T(4,128)S(1)}, f32[2,2,2,4,6912]{4,3,0,1,2:T(4,128)S(1)}, u32[]{:S(2)}, u32[]{:S(2)}) collective-permute-start(f32[2,2,2,4,6912]{4,3,0,1,2:T(4,128)S(1)} %select_bitcast_fusion.7), channel_id=1, source_target_pairs={{0,2},{1,3},{2,0},{3,1},{4,6},{5,7},{6,4},{7,5},{8,10},{9,11},{10,... | collective-permute-start | bytes 2654216 | tf_op jit(solution)/shard_map/ppermute | solution.py:29
  72.0 13.1 %collective-permute-start.2 = (f32[2,2,4,6912]{3,2,0,1:T(4,128)S(1)}, f32[2,2,4,6912]{3,2,0,1:T(4,128)S(1)}, u32[]{:S(2)}, u32[]{:S(2)}) collective-permute-start(f32[2,2,4,6912]{3,2,0,1:T(4,128)S(1)} %select_bitcast_fusion.12), channel_id=1, source_target_pairs={{0,4},{1,5},{2,6},{3,7},{4,0},{5,1},{6,2},{7,3},{8,12},{9,13},{10,... | collective-permute-start | bytes 1327112 | tf_op jit(solution)/shard_map/ppermute | solution.py:29
  85.4 6.0 %collective-permute-start.3 = (f32[2,4,6912]{2,1,0:T(4,128)S(1)}, f32[2,4,6912]{2,1,0:T(4,128)S(1)}, u32[]{:S(2)}, u32[]{:S(2)}) collective-permute-start(f32[2,4,6912]{2,1,0:T(4,128)S(1)} %select_bitcast_fusion.19), channel_id=1, source_target_pairs={{0,8},{1,9},{2,10},{3,11},{4,12},{5,13},{6,14},{7,15},{8,0},{9,1},... | collective-permute-start | bytes 663560 | tf_op jit(solution)/shard_map/ppermute | solution.py:29
  91.6 6.3 %collective-permute-start.4 = (f32[4,6912]{1,0:T(4,128)S(1)}, f32[4,6912]{1,0:T(4,128)S(1)}, u32[]{:S(2)}, u32[]{:S(2)}) collective-permute-start(f32[4,6912]{1,0:T(4,128)S(1)} %select_bitcast_fusion.28), channel_id=1, source_target_pairs={{0,16},{1,17},{2,18},{3,19},{4,20},{5,21},{6,22},{7,23},{8,24},{9,... | collective-permute-start | bytes 331784 | tf_op jit(solution)/shard_map/ppermute | solution.py:29
  103.2 5.4 %collective-permute-start.5 = (bf16[4,2304]{1,0:T(4,128)(2,1)S(1)}, bf16[4,2304]{1,0:T(4,128)(2,1)S(1)}, u32[]{:S(2)}, u32[]{:S(2)}) collective-permute-start(bf16[4,2304]{1,0:T(4,128)(2,1)S(1)} %convert_element_type.123), channel_id=1, source_target_pairs={{0,16},{1,17},{2,18},{3,19},{4,20},{5,21},{6,22},{7,23},{8,24},{9,... | collective-permute-start | bytes 55304 | tf_op jit(solution)/shard_map/ppermute | solution.py:29
  112.8 29.8 %collective-permute-start.7 = (bf16[2,2,4,2304]{3,2,1,0:T(4,128)(2,1)S(1)}, bf16[2,2,4,2304]{3,2,1,0:T(4,128)(2,1)S(1)}, u32[]{:S(2)}, u32[]{:S(2)}) collective-permute-start(bf16[2,2,4,2304]{3,2,1,0:T(4,128)(2,1)S(1)} %pad_maximum_fusion.14), channel_id=1, source_target_pairs={{0,4},{1,5},{2,6},{3,7},{4,0},{5,1},{6,2},{7,3},{8,12},{9,13},{10,... | collective-permute-start | bytes 221192 | tf_op jit(solution)/shard_map/ppermute | solution.py:29
  142.8 5.2 %collective-permute-start.8 = (bf16[2,2,2,4,2304]{4,3,2,1,0:T(4,128)(2,1)S(1)}, bf16[2,2,2,4,2304]{4,3,2,1,0:T(4,128)(2,1)S(1)}, u32[]{:S(2)}, u32[]{:S(2)}) collective-permute-start(bf16[2,2,2,4,2304]{4,3,2,1,0:T(4,128)(2,1)S(1)} %pad_maximum_fusion.11), channel_id=1, source_target_pairs={{0,2},{1,3},{2,0},{3,1},{4,6},{5,7},{6,4},{7,5},{8,10},{9,11},{10,... | collective-permute-start | bytes 442376 | tf_op jit(solution)/shard_map/ppermute | solution.py:29
  182.0 11.6 %collective-permute-start.10 = (f32[2,2,2,2,4,36,66]{6,4,5,3,2,1,0:T(4,128)}, f32[2,2,2,2,4,36,66]{6,4,5,3,2,1,0:T(4,128)S(1)}, u32[]{:S(2)}, u32[]{:S(2)}) collective-permute-start(f32[2,2,2,2,4,36,66]{6,4,5,3,2,1,0:T(4,128)} %copy.725), channel_id=1, source_target_pairs={{0,1},{1,0},{2,3},{3,2},{4,5},{5,4},{6,7},{7,6},{8,9},{9,8},{10,11... | collective-permute-start | bytes 1824776 | tf_op jit(solution)/shard_map/ppermute | solution.py:29
  208.4 15.5 %collective-permute-start.11 = (f32[2,2,2,4,36,66]{5,3,4,2,1,0:T(4,128)S(1)}, f32[2,2,2,4,36,66]{5,3,4,2,1,0:T(4,128)S(1)}, u32[]{:S(2)}, u32[]{:S(2)}) collective-permute-start(f32[2,2,2,4,36,66]{5,3,4,2,1,0:T(4,128)S(1)} %copy.729), channel_id=1, source_target_pairs={{0,2},{1,3},{2,0},{3,1},{4,6},{5,7},{6,4},{7,5},{8,10},{9,11},{10,... | collective-permute-start | bytes 912392 | tf_op jit(solution)/shard_map/ppermute | solution.py:29
  230.8 9.8 %collective-permute-start.12 = (f32[2,2,4,36,66]{4,2,3,1,0:T(4,128)S(1)}, f32[2,2,4,36,66]{4,2,3,1,0:T(4,128)S(1)}, u32[]{:S(2)}, u32[]{:S(2)}) collective-permute-start(f32[2,2,4,36,66]{4,2,3,1,0:T(4,128)S(1)} %copy.733), channel_id=1, source_target_pairs={{0,4},{1,5},{2,6},{3,7},{4,0},{5,1},{6,2},{7,3},{8,12},{9,13},{10,... | collective-permute-start | bytes 456200 | tf_op jit(solution)/shard_map/ppermute | solution.py:29
  242.1 6.9 %collective-permute-start.13 = (f32[2,4,36,66]{2,1,3,0:T(4,128)S(1)}, f32[2,4,36,66]{2,1,3,0:T(4,128)S(1)}, u32[]{:S(2)}, u32[]{:S(2)}) collective-permute-start(f32[2,4,36,66]{2,1,3,0:T(4,128)S(1)} %select_bitcast_fusion.18), channel_id=1, source_target_pairs={{0,8},{1,9},{2,10},{3,11},{4,12},{5,13},{6,14},{7,15},{8,0},{9,1},... | collective-permute-start | bytes 228104 | tf_op jit(solution)/shard_map/ppermute | solution.py:29
  249.3 6.6 %collective-permute-start.14 = (f32[4,36,66]{1,0,2:T(4,128)S(1)}, f32[4,36,66]{1,0,2:T(4,128)S(1)}, u32[]{:S(2)}, u32[]{:S(2)}) collective-permute-start(f32[4,36,66]{1,0,2:T(4,128)S(1)} %get-tuple-element.53), channel_id=1, source_target_pairs={{0,16},{1,17},{2,18},{3,19},{4,20},{5,21},{6,22},{7,23},{8,24},{9,... | collective-permute-start | bytes 114056 | tf_op jit(solution)/shard_map/ppermute | solution.py:29
  256.2 5.4 %collective-permute-start.15 = (bf16[4,2304]{1,0:T(4,128)(2,1)S(1)}, bf16[4,2304]{1,0:T(4,128)(2,1)S(1)}, u32[]{:S(2)}, u32[]{:S(2)}) collective-permute-start(bf16[4,2304]{1,0:T(4,128)(2,1)S(1)} %convert_element_type.126), channel_id=1, source_target_pairs={{0,16},{1,17},{2,18},{3,19},{4,20},{5,21},{6,22},{7,23},{8,24},{9,... | collective-permute-start | bytes 55304 | tf_op jit(solution)/shard_map/ppermute | solution.py:29
  265.8 6.2 %collective-permute-start.17 = (bf16[2,2,4,2304]{3,2,1,0:T(4,128)(2,1)S(1)}, bf16[2,2,4,2304]{3,2,1,0:T(4,128)(2,1)S(1)}, u32[]{:S(2)}, u32[]{:S(2)}) collective-permute-start(bf16[2,2,4,2304]{3,2,1,0:T(4,128)(2,1)S(1)} %pad_maximum_fusion.15), channel_id=1, source_target_pairs={{0,4},{1,5},{2,6},{3,7},{4,0},{5,1},{6,2},{7,3},{8,12},{9,13},{10,... | collective-permute-start | bytes 221192 | tf_op jit(solution)/shard_map/ppermute | solution.py:29
  272.1 5.2 %collective-permute-start.18 = (bf16[2,2,2,4,2304]{4,3,2,1,0:T(4,128)(2,1)S(1)}, bf16[2,2,2,4,2304]{4,3,2,1,0:T(4,128)(2,1)S(1)}, u32[]{:S(2)}, u32[]{:S(2)}) collective-permute-start(bf16[2,2,2,4,2304]{4,3,2,1,0:T(4,128)(2,1)S(1)} %pad_maximum_fusion.12), channel_id=1, source_target_pairs={{0,2},{1,3},{2,0},{3,1},{4,6},{5,7},{6,4},{7,5},{8,10},{9,11},{10,... | collective-permute-start | bytes 442376 | tf_op jit(solution)/shard_map/ppermute | solution.py:29
  324.6 5.9 %collective-permute-start.20 = (bf16[1,72,512]{2,1,0:T(8,128)(2,1)S(1)}, bf16[1,72,512]{2,1,0:T(8,128)(2,1)S(1)}, u32[]{:S(2)}, u32[]{:S(2)}) collective-permute-start(bf16[1,72,512]{2,1,0:T(8,128)(2,1)S(1)} %bitcast.344), channel_id=1, source_target_pairs={{0,16},{1,17},{2,18},{3,19},{4,20},{5,21},{6,22},{7,23},{8,24},{9,... | collective-permute-start | bytes 221192 | tf_op jit(solution)/shard_map/ppermute | solution.py:29
  330.6 5.2 %collective-permute-start.21 = (bf16[2,1,72,512]{3,2,0,1:T(8,128)(2,1)S(1)}, bf16[2,1,72,512]{3,2,0,1:T(8,128)(2,1)S(1)}, u32[]{:S(2)}, u32[]{:S(2)}) collective-permute-start(bf16[2,1,72,512]{3,2,0,1:T(8,128)(2,1)S(1)} %fusion.61), channel_id=1, source_target_pairs={{0,8},{1,9},{2,10},{3,11},{4,12},{5,13},{6,14},{7,15},{8,0},{9,1},... | collective-permute-start | bytes 442376 | tf_op jit(solution)/shard_map/ppermute | solution.py:29
  335.9 9.5 %collective-permute-start.22 = (bf16[2,2,1,72,512]{4,3,2,1,0:T(8,128)(2,1)S(1)}, bf16[2,2,1,72,512]{4,3,2,1,0:T(8,128)(2,1)S(1)}, u32[]{:S(2)}, u32[]{:S(2)}) collective-permute-start(bf16[2,2,1,72,512]{4,3,2,1,0:T(8,128)(2,1)S(1)} %fusion.54), channel_id=1, source_target_pairs={{0,4},{1,5},{2,6},{3,7},{4,0},{5,1},{6,2},{7,3},{8,12},{9,13},{10,... | collective-permute-start | bytes 884744 | tf_op jit(solution)/shard_map/ppermute | solution.py:29
  345.5 11.1 %collective-permute-start.23 = (bf16[2,2,2,1,72,512]{5,4,3,2,1,0:T(8,128)(2,1)S(1)}, bf16[2,2,2,1,72,512]{5,4,3,2,1,0:T(8,128)(2,1)S(1)}, u32[]{:S(2)}, u32[]{:S(2)}) collective-permute-start(bf16[2,2,2,1,72,512]{5,4,3,2,1,0:T(8,128)(2,1)S(1)} %fusion.39), channel_id=1, source_target_pairs={{0,2},{1,3},{2,0},{3,1},{4,6},{5,7},{6,4},{7,5},{8,10},{9,11},{10,... | collective-permute-start | bytes 1769480 | tf_op jit(solution)/shard_map/ppermute | solution.py:29
  374.0 28.1 %collective-permute-start.26 = (f32[2,2,2,72,512]{4,3,2,1,0:T(8,128)S(1)}, f32[2,2,2,72,512]{4,3,2,1,0:T(8,128)S(1)}, u32[]{:S(2)}, u32[]{:S(2)}) collective-permute-start(f32[2,2,2,72,512]{4,3,2,1,0:T(8,128)S(1)} %select_bitcast_fusion.3), channel_id=1, source_target_pairs={{0,2},{1,3},{2,0},{3,1},{4,6},{5,7},{6,4},{7,5},{8,10},{9,11},{10,... | collective-permute-start | bytes 3538952 | tf_op jit(solution)/shard_map/ppermute | solution.py:29
  402.6 16.1 %collective-permute-start.27 = (f32[2,2,72,512]{3,2,1,0:T(8,128)S(1)}, f32[2,2,72,512]{3,2,1,0:T(8,128)S(1)}, u32[]{:S(2)}, u32[]{:S(2)}) collective-permute-start(f32[2,2,72,512]{3,2,1,0:T(8,128)S(1)} %select_bitcast_fusion.8), channel_id=1, source_target_pairs={{0,4},{1,5},{2,6},{3,7},{4,0},{5,1},{6,2},{7,3},{8,12},{9,13},{10,... | collective-permute-start | bytes 1769480 | tf_op jit(solution)/shard_map/ppermute | solution.py:29
  418.9 7.4 %collective-permute-start.28 = (f32[2,72,512]{2,1,0:T(8,128)S(1)}, f32[2,72,512]{2,1,0:T(8,128)S(1)}, u32[]{:S(2)}, u32[]{:S(2)}) collective-permute-start(f32[2,72,512]{2,1,0:T(8,128)S(1)} %fusion.48), channel_id=1, source_target_pairs={{0,8},{1,9},{2,10},{3,11},{4,12},{5,13},{6,14},{7,15},{8,0},{9,1},... | collective-permute-start | bytes 884744 | tf_op jit(solution)/shard_map/ppermute | solution.py:29
  426.4 6.7 %collective-permute-start.29 = (f32[72,512]{1,0:T(8,128)S(1)}, f32[72,512]{1,0:T(8,128)S(1)}, u32[]{:S(2)}, u32[]{:S(2)}) collective-permute-start(f32[72,512]{1,0:T(8,128)S(1)} %select_bitcast_fusion.20), channel_id=1, source_target_pairs={{0,16},{1,17},{2,18},{3,19},{4,20},{5,21},{6,22},{7,23},{8,24},{9,... | collective-permute-start | bytes 442376 | tf_op jit(solution)/shard_map/ppermute | solution.py:29
  436.2 11.7 %all-to-all-start.1 = ((bf16[8,2,2304]{2,1,0:T(2,128)(2,1)}), bf16[8,2,2304]{2,1,0:T(2,128)(2,1)S(1)}, u32[]{:S(2)}, u32[]{:S(2)}) async-start(bf16[8,2,2304]{2,1,0:T(2,128)(2,1)} %reshape.416), calls=%async_computation.1 | async-start | bytes 147456 | tf_op jit(solution)/shard_map/all_to_all | solution.py:341
  (28 other events, 451.7 us)
